TPU v7x, 256 devices: a whole 4x4x8 slice. The times are simulated.
256 devices in a mesh: run: 2 (over core), ctx: 32 (over x, z), head: 4 (over y).
Axes of the slice: x: 4, y: 4, z: 8, core: 2. Of those that a mesh axis runs over, the one named last changes fastest.
Arguments:
- inner_tokens: bfloat16 [131072, 5120], P(('run', 'ctx', 'head')), parts along dimension 0, may hold values from -6 to 6
- state_inputs: bfloat16 [131072, 256], P(('run', 'ctx', 'head')), parts along dimension 0, may hold values from -6 to 6
- step_raw: bfloat16 [131072, 80], P(('run', 'ctx', 'head')), parts along dimension 0, may hold values from -3 to 24
- conv_inner: float32 [5, 5120], P(None, 'head'), may hold values from -3 to 3
- conv_state: float32 [5, 256], replicated, may hold values from -3 to 3
- head_rates: float32 [4, 80], P('run', 'head'), parts along dimension 0, may hold values from -15 to 4
- skip_gain: float32 [80], P('head'), may hold values from 0.5 to 1.5
Outputs:
- mixed: bfloat16 [131072, 5120], P(('run', 'ctx', 'head')), parts along dimension 0
There are 2 independent parts, one for each index of `run`. A program takes and returns all parts, laid end to end along the dimension named above; an argument that names none is the same for every part. Nothing has to cross between parts.
All inputs are finite; a program needn't handle non-finite values.
Results may differ from a plain program's by a relative error of at most 0.009.
Values may be sent and summed in bfloat16 or wider, within the bound.
No kernel may reach another device: no remote copies, remote signals or barrier semaphores. Data moves between devices by JAX's collectives and lax.ppermute only.
A program may use at most 192 MiB of HBM per device.

v0:
```python
import jax
import jax.numpy as jnp
from jax import lax
from jax.sharding import PartitionSpec as P

KERNEL = 4
SPAN = 256


def from_behind(value, axis, by):
    length = lax.axis_size(axis)
    pairs = [(i, i + by) for i in range(length) if 0 <= i + by < length]
    return lax.ppermute(value, axis, pairs)


def silu_conv(signal, previous_rows, kernel_taps):
    length = signal.shape[0]
    channels = signal.shape[1]
    padded = jnp.concatenate(
        [previous_rows.astype(jnp.float32), signal.astype(jnp.float32)], axis=0
    )
    summed = jnp.zeros((length, channels), jnp.float32) + kernel_taps[KERNEL][None, :]
    for offset in range(KERNEL):
        summed = summed + kernel_taps[offset][None, :] * padded[offset : offset + length]
    return jax.nn.silu(summed).astype(jnp.bfloat16)


def block_terms(carry_state, pieces):
    c_block, b_block, u_block, decay_block = pieces
    cumulative = jnp.cumsum(decay_block, axis=0)
    across = cumulative.T
    inner_scores = jnp.dot(c_block, b_block.T, preferred_element_type=jnp.float32)
    spread = across[:, :, None] - across[:, None, :]
    places = jnp.arange(c_block.shape[0])
    causal = places[:, None] >= places[None, :]
    mixing = (inner_scores[None] * jnp.exp(jnp.where(causal[None], spread, -jnp.inf))).astype(
        jnp.bfloat16
    )
    local_terms = jnp.einsum("hts,shp->thp", mixing, u_block, preferred_element_type=jnp.float32)
    carried = jnp.exp(cumulative)[:, :, None] * jnp.einsum(
        "tn,hpn->thp", c_block.astype(jnp.float32), carry_state, precision=lax.Precision.HIGHEST
    )
    ending = cumulative[-1]
    weights = jnp.exp(ending[None, :] - cumulative)
    scaled = weights[:, :, None] * u_block.astype(jnp.float32)
    new_state = jnp.exp(ending)[:, None, None] * carry_state + jnp.einsum(
        "shp,sn->hpn", scaled, b_block.astype(jnp.float32), precision=lax.Precision.HIGHEST
    )
    return (new_state, local_terms + carried)


def per_device(inner_tokens, state_inputs, step_raw, conv_inner, conv_state, head_rates, skip_gain):
    x_local, step_local = (
        lax.all_to_all(inner_tokens, "head", split_axis=1, concat_axis=0, tiled=True),
        lax.all_to_all(step_raw, "head", split_axis=1, concat_axis=0, tiled=True),
    )
    context = x_local.shape[0]
    channels = x_local.shape[1]
    heads_local = head_rates.shape[1]
    head_width = channels // heads_local
    margin_rows = KERNEL - 1
    state_whole = lax.all_gather(state_inputs, "head", axis=0, tiled=True)
    edge_rows = jnp.concatenate(
        [x_local[context - margin_rows :], state_whole[context - margin_rows :]], axis=1
    )
    previous_rows = from_behind(edge_rows, "ctx", 1)
    x_previous = previous_rows[:, :channels]
    state_conv = silu_conv(state_whole, previous_rows[:, channels:], conv_state)
    inner_conv = silu_conv(x_local, x_previous, conv_inner)
    state_width = state_conv.shape[1] // 2
    b_rows = state_conv[:, :state_width]
    c_rows = state_conv[:, state_width:]
    step_size = jax.nn.softplus(step_local.astype(jnp.float32) + head_rates[0][None, :])
    log_decay = -step_size * jnp.exp(head_rates[1])[None, :]
    x_heads = inner_conv.reshape(context, heads_local, head_width)
    inputs = (x_heads.astype(jnp.float32) * step_size[:, :, None]).astype(jnp.bfloat16)
    block_count = context // SPAN
    start_state = jnp.zeros((heads_local, head_width, state_width), jnp.float32)
    final_state, outputs = lax.scan(
        block_terms,
        start_state,
        (
            c_rows.reshape(block_count, SPAN, state_width),
            b_rows.reshape(block_count, SPAN, state_width),
            inputs.reshape(block_count, SPAN, heads_local, head_width),
            log_decay.reshape(block_count, SPAN, heads_local),
        ),
    )
    running = jnp.cumsum(log_decay, axis=0)
    device_decay = jnp.exp(running[-1])

    def relay(position, arriving):
        return from_behind(device_decay[:, None, None] * arriving + final_state, "ctx", 1)

    incoming = lax.fori_loop(0, lax.axis_size("ctx") - 1, relay, jnp.zeros_like(final_state))
    carried = jnp.exp(running)[:, :, None] * jnp.einsum(
        "tn,hpn->thp", c_rows.astype(jnp.float32), incoming, precision=lax.Precision.HIGHEST
    )
    summed = (
        outputs.reshape(context, heads_local, head_width)
        + carried
        + skip_gain[None, :, None] * x_heads.astype(jnp.float32)
    )
    regrouped = summed.astype(jnp.bfloat16).reshape(context, channels)
    return lax.all_to_all(regrouped, "head", split_axis=0, concat_axis=1, tiled=True)


def solution(mesh):
    return jax.shard_map(
        per_device,
        mesh=mesh,
        in_specs=(
            P(("run", "ctx", "head"), None),
            P(("run", "ctx", "head"), None),
            P(("run", "ctx", "head"), None),
            P(None, "head"),
            P(),
            P("run", "head"),
            P("head"),
        ),
        out_specs=P(("run", "ctx", "head"), None),
        check_vma=False,
    )
```

profile of v0, /device:TPU:6, one launch (start us, length us, event | category | flops | bytes accessed | tf_op | source)
XLA Modules:
  0.0 1098.5 jit_solution(2019038271376231881)
XLA Ops:
  31.9 30.6 %all-gather.2.cloned.1.call-done = bf16[2048,256]{1,0:T(8,128)(2,1)} async-done(((bf16[512,256]{1,0:T(8,128)(2,1)}), bf16[2048,256]{1,0:T(8,128)(2,1)}) %all-gather.2.cloned.1.call-update) | async-done | bytes 1048592 | tf_op jit(solution)/shard_map/all_gather | solution.py:62
  64.6 26.9 %all-to-all-done.1 = bf16[512,4,1280]{2,0,1:T(8,128)(2,1)} async-done(((bf16[512,4,1280]{2,0,1:T(8,128)(2,1)}), bf16[512,4,1280]{2,0,1:T(8,128)(2,1)}, u32[]{:S(2)}, u32[]{:S(2)}) %all-to-all-start.1) | async-done | bytes 5242912 | tf_op jit(solution)/shard_map/all_to_all | solution.py:54
  110.1 11.4 %copy.83 = f32[2048,1280]{0,1:T(8,128)} copy(f32[2048,1280]{1,0:T(8,128)} %fusion.47) | data formatting | bytes 20971520 | tf_op jit(solution)/shard_map/convert_element_type | solution.py:76
  121.5 9.2 copy.101
  142.9 307.2 %while.24 = (s32[]{:T(128)}, f32[20,64,128]{2,1,0:T(8,128)S(1)}, f32[8,256,20,64]{1,0,3,2:T(8,128)}, f32[8,256,20]{1,0,2:T(8,128)S(1)}, bf16[8,256,20,64]{1,3,2,...) while((s32[]{:T(128)}, f32[20,64,128]{2,1,0:T(8,128)S(1)}, ...), condition=%wide.region_3.4_spmd.clone, body=%wide.region_0.3_spmd.clone.sunk | while | flops 1199117312 | bytes 13914835 | solution.py:79
  151.5 30.0 %dynamic_update_slice.6 = f32[8,256,20,64]{1,0,3,2:T(8,128)} dynamic-update-slice(f32[8,256,20,64]{1,0,3,2:T(8,128)} %get-tuple-element.251, f32[1,256,20,64]{1,0,3,2:T(1,128)S(1)} %copy.120, s32[]{:T(128)S(6)} %copy.125, s32[]{:T(128)} %constant.36.clone.1..sunk, s32[]{:T(128)} %constant.36.clone.1..sunk, s32[]{:T(128)} %constant.36.clone.1..sunk) | dynamic-update-slice | bytes 2621444 | tf_op jit(solution)/shard_map/while/body/jit(dynamic_update_index_in_dim)/dynamic_update_slice | solution.py:79
  189.9 30.0 %dynamic_update_slice.6 = f32[8,256,20,64]{1,0,3,2:T(8,128)} dynamic-update-slice(f32[8,256,20,64]{1,0,3,2:T(8,128)} %get-tuple-element.251, f32[1,256,20,64]{1,0,3,2:T(1,128)S(1)} %copy.120, s32[]{:T(128)S(6)} %copy.125, s32[]{:T(128)} %constant.36.clone.1..sunk, s32[]{:T(128)} %constant.36.clone.1..sunk, s32[]{:T(128)} %constant.36.clone.1..sunk) | dynamic-update-slice | bytes 2621444 | tf_op jit(solution)/shard_map/while/body/jit(dynamic_update_index_in_dim)/dynamic_update_slice | solution.py:79
  228.2 30.0 %dynamic_update_slice.6 = f32[8,256,20,64]{1,0,3,2:T(8,128)} dynamic-update-slice(f32[8,256,20,64]{1,0,3,2:T(8,128)} %get-tuple-element.251, f32[1,256,20,64]{1,0,3,2:T(1,128)S(1)} %copy.120, s32[]{:T(128)S(6)} %copy.125, s32[]{:T(128)} %constant.36.clone.1..sunk, s32[]{:T(128)} %constant.36.clone.1..sunk, s32[]{:T(128)} %constant.36.clone.1..sunk) | dynamic-update-slice | bytes 2621444 | tf_op jit(solution)/shard_map/while/body/jit(dynamic_update_index_in_dim)/dynamic_update_slice | solution.py:79
  266.6 30.0 %dynamic_update_slice.6 = f32[8,256,20,64]{1,0,3,2:T(8,128)} dynamic-update-slice(f32[8,256,20,64]{1,0,3,2:T(8,128)} %get-tuple-element.251, f32[1,256,20,64]{1,0,3,2:T(1,128)S(1)} %copy.120, s32[]{:T(128)S(6)} %copy.125, s32[]{:T(128)} %constant.36.clone.1..sunk, s32[]{:T(128)} %constant.36.clone.1..sunk, s32[]{:T(128)} %constant.36.clone.1..sunk) | dynamic-update-slice | bytes 2621444 | tf_op jit(solution)/shard_map/while/body/jit(dynamic_update_index_in_dim)/dynamic_update_slice | solution.py:79
  305.0 30.0 %dynamic_update_slice.6 = f32[8,256,20,64]{1,0,3,2:T(8,128)} dynamic-update-slice(f32[8,256,20,64]{1,0,3,2:T(8,128)} %get-tuple-element.251, f32[1,256,20,64]{1,0,3,2:T(1,128)S(1)} %copy.120, s32[]{:T(128)S(6)} %copy.125, s32[]{:T(128)} %constant.36.clone.1..sunk, s32[]{:T(128)} %constant.36.clone.1..sunk, s32[]{:T(128)} %constant.36.clone.1..sunk) | dynamic-update-slice | bytes 2621444 | tf_op jit(solution)/shard_map/while/body/jit(dynamic_update_index_in_dim)/dynamic_update_slice | solution.py:79
  343.3 30.0 %dynamic_update_slice.6 = f32[8,256,20,64]{1,0,3,2:T(8,128)} dynamic-update-slice(f32[8,256,20,64]{1,0,3,2:T(8,128)} %get-tuple-element.251, f32[1,256,20,64]{1,0,3,2:T(1,128)S(1)} %copy.120, s32[]{:T(128)S(6)} %copy.125, s32[]{:T(128)} %constant.36.clone.1..sunk, s32[]{:T(128)} %constant.36.clone.1..sunk, s32[]{:T(128)} %constant.36.clone.1..sunk) | dynamic-update-slice | bytes 2621444 | tf_op jit(solution)/shard_map/while/body/jit(dynamic_update_index_in_dim)/dynamic_update_slice | solution.py:79
  381.7 30.0 %dynamic_update_slice.6 = f32[8,256,20,64]{1,0,3,2:T(8,128)} dynamic-update-slice(f32[8,256,20,64]{1,0,3,2:T(8,128)} %get-tuple-element.251, f32[1,256,20,64]{1,0,3,2:T(1,128)S(1)} %copy.120, s32[]{:T(128)S(6)} %copy.125, s32[]{:T(128)} %constant.36.clone.1..sunk, s32[]{:T(128)} %constant.36.clone.1..sunk, s32[]{:T(128)} %constant.36.clone.1..sunk) | dynamic-update-slice | bytes 2621444 | tf_op jit(solution)/shard_map/while/body/jit(dynamic_update_index_in_dim)/dynamic_update_slice | solution.py:79
  420.1 30.0 %dynamic_update_slice.6 = f32[8,256,20,64]{1,0,3,2:T(8,128)} dynamic-update-slice(f32[8,256,20,64]{1,0,3,2:T(8,128)} %get-tuple-element.251, f32[1,256,20,64]{1,0,3,2:T(1,128)S(1)} %copy.120, s32[]{:T(128)S(6)} %copy.125, s32[]{:T(128)} %constant.36.clone.1..sunk, s32[]{:T(128)} %constant.36.clone.1..sunk, s32[]{:T(128)} %constant.36.clone.1..sunk) | dynamic-update-slice | bytes 2621444 | tf_op jit(solution)/shard_map/while/body/jit(dynamic_update_index_in_dim)/dynamic_update_slice | solution.py:79
  450.1 11.4 %reshape.140 = f32[2048,20,64]{0,2,1:T(8,128)} reshape(f32[8,256,20,64]{1,0,3,2:T(8,128)} %get-tuple-element.65) | data formatting | bytes 20971520 | tf_op jit(solution)/shard_map/reshape | solution.py:100
  461.6 559.1 %while.23 = (s32[]{:T(128)}, f32[20,64,128]{2,1,0:T(8,128)S(1)}, f32[20]{0:T(128)S(1)}, f32[20,64,128]{2,1,0:T(8,128)S(1)}, s32[]{:T(128)}) while((s32[]{:T(128)}, f32[20,64,128]{2,1,0:T(8,128)S(1)}, f32[20]{0:T(128)S(1)}, f32[20,64,128]{2,1,0:T(8,128)S(1)}, s32[]{:T(128)}) %tuple.57), condition=%wide.region_7.8_spmd, body=%wide.region_6.7_spmd.sunk | while | flops 327682 | bytes 4587701 | solution.py:95
  463.8 16.0 %collective-permute-done = f32[20,64,128]{2,1,0:T(8,128)S(1)} collective-permute-done((f32[20,64,128]{2,1,0:T(8,128)S(1)}, f32[20,64,128]{2,1,0:T(8,128)S(1)}, u32[]{:S(2)}, u32[]{:S(2)}) %collective-permute-start) | collective-permute-done | bytes 655392 | tf_op jit(solution)/shard_map/while/body/eval_jaxpr/ppermute | solution.py:13
  481.8 15.1 %collective-permute-done = f32[20,64,128]{2,1,0:T(8,128)S(1)} collective-permute-done((f32[20,64,128]{2,1,0:T(8,128)S(1)}, f32[20,64,128]{2,1,0:T(8,128)S(1)}, u32[]{:S(2)}, u32[]{:S(2)}) %collective-permute-start) | collective-permute-done | bytes 655392 | tf_op jit(solution)/shard_map/while/body/eval_jaxpr/ppermute | solution.py:13
  499.0 14.2 %collective-permute-done = f32[20,64,128]{2,1,0:T(8,128)S(1)} collective-permute-done((f32[20,64,128]{2,1,0:T(8,128)S(1)}, f32[20,64,128]{2,1,0:T(8,128)S(1)}, u32[]{:S(2)}, u32[]{:S(2)}) %collective-permute-start) | collective-permute-done | bytes 655392 | tf_op jit(solution)/shard_map/while/body/eval_jaxpr/ppermute | solution.py:13
  515.3 13.4 %collective-permute-done = f32[20,64,128]{2,1,0:T(8,128)S(1)} collective-permute-done((f32[20,64,128]{2,1,0:T(8,128)S(1)}, f32[20,64,128]{2,1,0:T(8,128)S(1)}, u32[]{:S(2)}, u32[]{:S(2)}) %collective-permute-start) | collective-permute-done | bytes 655392 | tf_op jit(solution)/shard_map/while/body/eval_jaxpr/ppermute | solution.py:13
  530.7 13.3 %collective-permute-done = f32[20,64,128]{2,1,0:T(8,128)S(1)} collective-permute-done((f32[20,64,128]{2,1,0:T(8,128)S(1)}, f32[20,64,128]{2,1,0:T(8,128)S(1)}, u32[]{:S(2)}, u32[]{:S(2)}) %collective-permute-start) | collective-permute-done | bytes 655392 | tf_op jit(solution)/shard_map/while/body/eval_jaxpr/ppermute | solution.py:13
  546.1 14.4 %collective-permute-done = f32[20,64,128]{2,1,0:T(8,128)S(1)} collective-permute-done((f32[20,64,128]{2,1,0:T(8,128)S(1)}, f32[20,64,128]{2,1,0:T(8,128)S(1)}, u32[]{:S(2)}, u32[]{:S(2)}) %collective-permute-start) | collective-permute-done | bytes 655392 | tf_op jit(solution)/shard_map/while/body/eval_jaxpr/ppermute | solution.py:13
  562.5 15.5 %collective-permute-done = f32[20,64,128]{2,1,0:T(8,128)S(1)} collective-permute-done((f32[20,64,128]{2,1,0:T(8,128)S(1)}, f32[20,64,128]{2,1,0:T(8,128)S(1)}, u32[]{:S(2)}, u32[]{:S(2)}) %collective-permute-start) | collective-permute-done | bytes 655392 | tf_op jit(solution)/shard_map/while/body/eval_jaxpr/ppermute | solution.py:13
  580.1 16.7 %collective-permute-done = f32[20,64,128]{2,1,0:T(8,128)S(1)} collective-permute-done((f32[20,64,128]{2,1,0:T(8,128)S(1)}, f32[20,64,128]{2,1,0:T(8,128)S(1)}, u32[]{:S(2)}, u32[]{:S(2)}) %collective-permute-start) | collective-permute-done | bytes 655392 | tf_op jit(solution)/shard_map/while/body/eval_jaxpr/ppermute | solution.py:13
  598.9 17.8 %collective-permute-done = f32[20,64,128]{2,1,0:T(8,128)S(1)} collective-permute-done((f32[20,64,128]{2,1,0:T(8,128)S(1)}, f32[20,64,128]{2,1,0:T(8,128)S(1)}, u32[]{:S(2)}, u32[]{:S(2)}) %collective-permute-start) | collective-permute-done | bytes 655392 | tf_op jit(solution)/shard_map/while/body/eval_jaxpr/ppermute | solution.py:13
  618.8 19.0 %collective-permute-done = f32[20,64,128]{2,1,0:T(8,128)S(1)} collective-permute-done((f32[20,64,128]{2,1,0:T(8,128)S(1)}, f32[20,64,128]{2,1,0:T(8,128)S(1)}, u32[]{:S(2)}, u32[]{:S(2)}) %collective-permute-start) | collective-permute-done | bytes 655392 | tf_op jit(solution)/shard_map/while/body/eval_jaxpr/ppermute | solution.py:13
  639.9 19.2 %collective-permute-done = f32[20,64,128]{2,1,0:T(8,128)S(1)} collective-permute-done((f32[20,64,128]{2,1,0:T(8,128)S(1)}, f32[20,64,128]{2,1,0:T(8,128)S(1)}, u32[]{:S(2)}, u32[]{:S(2)}) %collective-permute-start) | collective-permute-done | bytes 655392 | tf_op jit(solution)/shard_map/while/body/eval_jaxpr/ppermute | solution.py:13
  661.1 18.4 %collective-permute-done = f32[20,64,128]{2,1,0:T(8,128)S(1)} collective-permute-done((f32[20,64,128]{2,1,0:T(8,128)S(1)}, f32[20,64,128]{2,1,0:T(8,128)S(1)}, u32[]{:S(2)}, u32[]{:S(2)}) %collective-permute-start) | collective-permute-done | bytes 655392 | tf_op jit(solution)/shard_map/while/body/eval_jaxpr/ppermute | solution.py:13
  681.6 17.5 %collective-permute-done = f32[20,64,128]{2,1,0:T(8,128)S(1)} collective-permute-done((f32[20,64,128]{2,1,0:T(8,128)S(1)}, f32[20,64,128]{2,1,0:T(8,128)S(1)}, u32[]{:S(2)}, u32[]{:S(2)}) %collective-permute-start) | collective-permute-done | bytes 655392 | tf_op jit(solution)/shard_map/while/body/eval_jaxpr/ppermute | solution.py:13
  701.1 16.7 %collective-permute-done = f32[20,64,128]{2,1,0:T(8,128)S(1)} collective-permute-done((f32[20,64,128]{2,1,0:T(8,128)S(1)}, f32[20,64,128]{2,1,0:T(8,128)S(1)}, u32[]{:S(2)}, u32[]{:S(2)}) %collective-permute-start) | collective-permute-done | bytes 655392 | tf_op jit(solution)/shard_map/while/body/eval_jaxpr/ppermute | solution.py:13
  719.9 15.8 %collective-permute-done = f32[20,64,128]{2,1,0:T(8,128)S(1)} collective-permute-done((f32[20,64,128]{2,1,0:T(8,128)S(1)}, f32[20,64,128]{2,1,0:T(8,128)S(1)}, u32[]{:S(2)}, u32[]{:S(2)}) %collective-permute-start) | collective-permute-done | bytes 655392 | tf_op jit(solution)/shard_map/while/body/eval_jaxpr/ppermute | solution.py:13
  737.7 14.9 %collective-permute-done = f32[20,64,128]{2,1,0:T(8,128)S(1)} collective-permute-done((f32[20,64,128]{2,1,0:T(8,128)S(1)}, f32[20,64,128]{2,1,0:T(8,128)S(1)}, u32[]{:S(2)}, u32[]{:S(2)}) %collective-permute-start) | collective-permute-done | bytes 655392 | tf_op jit(solution)/shard_map/while/body/eval_jaxpr/ppermute | solution.py:13
  754.7 14.1 %collective-permute-done = f32[20,64,128]{2,1,0:T(8,128)S(1)} collective-permute-done((f32[20,64,128]{2,1,0:T(8,128)S(1)}, f32[20,64,128]{2,1,0:T(8,128)S(1)}, u32[]{:S(2)}, u32[]{:S(2)}) %collective-permute-start) | collective-permute-done | bytes 655392 | tf_op jit(solution)/shard_map/while/body/eval_jaxpr/ppermute | solution.py:13
  770.9 13.2 %collective-permute-done = f32[20,64,128]{2,1,0:T(8,128)S(1)} collective-permute-done((f32[20,64,128]{2,1,0:T(8,128)S(1)}, f32[20,64,128]{2,1,0:T(8,128)S(1)}, u32[]{:S(2)}, u32[]{:S(2)}) %collective-permute-start) | collective-permute-done | bytes 655392 | tf_op jit(solution)/shard_map/while/body/eval_jaxpr/ppermute | solution.py:13
  786.2 13.4 %collective-permute-done = f32[20,64,128]{2,1,0:T(8,128)S(1)} collective-permute-done((f32[20,64,128]{2,1,0:T(8,128)S(1)}, f32[20,64,128]{2,1,0:T(8,128)S(1)}, u32[]{:S(2)}, u32[]{:S(2)}) %collective-permute-start) | collective-permute-done | bytes 655392 | tf_op jit(solution)/shard_map/while/body/eval_jaxpr/ppermute | solution.py:13
  801.7 14.6 %collective-permute-done = f32[20,64,128]{2,1,0:T(8,128)S(1)} collective-permute-done((f32[20,64,128]{2,1,0:T(8,128)S(1)}, f32[20,64,128]{2,1,0:T(8,128)S(1)}, u32[]{:S(2)}, u32[]{:S(2)}) %collective-permute-start) | collective-permute-done | bytes 655392 | tf_op jit(solution)/shard_map/while/body/eval_jaxpr/ppermute | solution.py:13
  818.3 15.7 %collective-permute-done = f32[20,64,128]{2,1,0:T(8,128)S(1)} collective-permute-done((f32[20,64,128]{2,1,0:T(8,128)S(1)}, f32[20,64,128]{2,1,0:T(8,128)S(1)}, u32[]{:S(2)}, u32[]{:S(2)}) %collective-permute-start) | collective-permute-done | bytes 655392 | tf_op jit(solution)/shard_map/while/body/eval_jaxpr/ppermute | solution.py:13
  836.0 16.8 %collective-permute-done = f32[20,64,128]{2,1,0:T(8,128)S(1)} collective-permute-done((f32[20,64,128]{2,1,0:T(8,128)S(1)}, f32[20,64,128]{2,1,0:T(8,128)S(1)}, u32[]{:S(2)}, u32[]{:S(2)}) %collective-permute-start) | collective-permute-done | bytes 655392 | tf_op jit(solution)/shard_map/while/body/eval_jaxpr/ppermute | solution.py:13
  855.0 18.0 %collective-permute-done = f32[20,64,128]{2,1,0:T(8,128)S(1)} collective-permute-done((f32[20,64,128]{2,1,0:T(8,128)S(1)}, f32[20,64,128]{2,1,0:T(8,128)S(1)}, u32[]{:S(2)}, u32[]{:S(2)}) %collective-permute-start) | collective-permute-done | bytes 655392 | tf_op jit(solution)/shard_map/while/body/eval_jaxpr/ppermute | solution.py:13
  875.0 19.1 %collective-permute-done = f32[20,64,128]{2,1,0:T(8,128)S(1)} collective-permute-done((f32[20,64,128]{2,1,0:T(8,128)S(1)}, f32[20,64,128]{2,1,0:T(8,128)S(1)}, u32[]{:S(2)}, u32[]{:S(2)}) %collective-permute-start) | collective-permute-done | bytes 655392 | tf_op jit(solution)/shard_map/while/body/eval_jaxpr/ppermute | solution.py:13
  896.2 19.1 %collective-permute-done = f32[20,64,128]{2,1,0:T(8,128)S(1)} collective-permute-done((f32[20,64,128]{2,1,0:T(8,128)S(1)}, f32[20,64,128]{2,1,0:T(8,128)S(1)}, u32[]{:S(2)}, u32[]{:S(2)}) %collective-permute-start) | collective-permute-done | bytes 655392 | tf_op jit(solution)/shard_map/while/body/eval_jaxpr/ppermute | solution.py:13
  917.4 18.2 %collective-permute-done = f32[20,64,128]{2,1,0:T(8,128)S(1)} collective-permute-done((f32[20,64,128]{2,1,0:T(8,128)S(1)}, f32[20,64,128]{2,1,0:T(8,128)S(1)}, u32[]{:S(2)}, u32[]{:S(2)}) %collective-permute-start) | collective-permute-done | bytes 655392 | tf_op jit(solution)/shard_map/while/body/eval_jaxpr/ppermute | solution.py:13
  937.6 17.4 %collective-permute-done = f32[20,64,128]{2,1,0:T(8,128)S(1)} collective-permute-done((f32[20,64,128]{2,1,0:T(8,128)S(1)}, f32[20,64,128]{2,1,0:T(8,128)S(1)}, u32[]{:S(2)}, u32[]{:S(2)}) %collective-permute-start) | collective-permute-done | bytes 655392 | tf_op jit(solution)/shard_map/while/body/eval_jaxpr/ppermute | solution.py:13
  957.0 16.5 %collective-permute-done = f32[20,64,128]{2,1,0:T(8,128)S(1)} collective-permute-done((f32[20,64,128]{2,1,0:T(8,128)S(1)}, f32[20,64,128]{2,1,0:T(8,128)S(1)}, u32[]{:S(2)}, u32[]{:S(2)}) %collective-permute-start) | collective-permute-done | bytes 655392 | tf_op jit(solution)/shard_map/while/body/eval_jaxpr/ppermute | solution.py:13
  975.6 15.6 %collective-permute-done = f32[20,64,128]{2,1,0:T(8,128)S(1)} collective-permute-done((f32[20,64,128]{2,1,0:T(8,128)S(1)}, f32[20,64,128]{2,1,0:T(8,128)S(1)}, u32[]{:S(2)}, u32[]{:S(2)}) %collective-permute-start) | collective-permute-done | bytes 655392 | tf_op jit(solution)/shard_map/while/body/eval_jaxpr/ppermute | solution.py:13
  993.3 12.7 %collective-permute-done = f32[20,64,128]{2,1,0:T(8,128)S(1)} collective-permute-done((f32[20,64,128]{2,1,0:T(8,128)S(1)}, f32[20,64,128]{2,1,0:T(8,128)S(1)}, u32[]{:S(2)}, u32[]{:S(2)}) %collective-permute-start) | collective-permute-done | bytes 655392 | tf_op jit(solution)/shard_map/while/body/eval_jaxpr/ppermute | solution.py:13
  1008.0 12.7 %collective-permute-done = f32[20,64,128]{2,1,0:T(8,128)S(1)} collective-permute-done((f32[20,64,128]{2,1,0:T(8,128)S(1)}, f32[20,64,128]{2,1,0:T(8,128)S(1)}, u32[]{:S(2)}, u32[]{:S(2)}) %collective-permute-start) | collective-permute-done | bytes 655392 | tf_op jit(solution)/shard_map/while/body/eval_jaxpr/ppermute | solution.py:13
  1033.9 9.5 all_to_all.44
  1046.9 36.9 %all_to_all.51 = bf16[4,512,1280]{1,2,0:T(8,128)(2,1)} all-to-all(bf16[4,512,1280]{1,2,0:T(8,128)(2,1)S(1)} %copy.91), channel_id=1, replica_groups=mesh['run'=2,'ctx'=32,'head'=4] {'head'}, dimensions={0} | all-to-all | bytes 10485760 | tf_op jit(solution)/shard_map/all_to_all | solution.py:105
  (294 shorter events, 212.1 us)
Async XLA Ops:
  8.1 10.3 all-to-all-start
  18.3 5.9 copy-start.3
  18.3 6.0 copy-start.5
  18.3 6.1 copy-start.4
  18.3 73.1 %all-to-all-start.1 = ((bf16[512,4,1280]{2,0,1:T(8,128)(2,1)}), bf16[512,4,1280]{2,0,1:T(8,128)(2,1)}, u32[]{:S(2)}, u32[]{:S(2)}) async-start(bf16[512,4,1280]{2,0,1:T(8,128)(2,1)} %bitcast.129), calls=%async_computation.1 | async-start | bytes 10485760 | tf_op jit(solution)/shard_map/all_to_all | solution.py:54
  23.5 39.0 %all-gather.2.cloned.1.call-start = ((), (), s32[]{:S(2)}) async-start(), calls=%async_computation.3 | async-start | bytes 1310720 | tf_op jit(solution)/shard_map/all_gather | solution.py:62
  92.2 9.7 collective-permute-start.1
  141.9 1.0 copy-start.1
  461.5 559.2 %copy-start.2 = (bf16[2048,256]{1,0:T(8,128)(2,1)S(1)}, bf16[2048,256]{1,0:T(8,128)(2,1)}, u32[]{:S(2)}) copy-start(bf16[2048,256]{1,0:T(8,128)(2,1)} %copy-done.1) | copy-start | bytes 3145732
  461.7 18.0 %collective-permute-start = (f32[20,64,128]{2,1,0:T(8,128)S(1)}, f32[20,64,128]{2,1,0:T(8,128)S(1)}, u32[]{:S(2)}, u32[]{:S(2)}) collective-permute-start(f32[20,64,128]{2,1,0:T(8,128)S(1)} %multiply_add_fusion.2), channel_id=1, source_target_pairs={{0,4},{4,8},{8,12},{12,16},{16,20},{20,24},{24,28},{28,32},{32,36}... | collective-permute-start | bytes 1966088 | tf_op jit(solution)/shard_map/while/body/eval_jaxpr/ppermute | solution.py:13
  479.9 17.0 %collective-permute-start = (f32[20,64,128]{2,1,0:T(8,128)S(1)}, f32[20,64,128]{2,1,0:T(8,128)S(1)}, u32[]{:S(2)}, u32[]{:S(2)}) collective-permute-start(f32[20,64,128]{2,1,0:T(8,128)S(1)} %multiply_add_fusion.2), channel_id=1, source_target_pairs={{0,4},{4,8},{8,12},{12,16},{16,20},{20,24},{24,28},{28,32},{32,36}... | collective-permute-start | bytes 1966088 | tf_op jit(solution)/shard_map/while/body/eval_jaxpr/ppermute | solution.py:13
  497.1 16.2 %collective-permute-start = (f32[20,64,128]{2,1,0:T(8,128)S(1)}, f32[20,64,128]{2,1,0:T(8,128)S(1)}, u32[]{:S(2)}, u32[]{:S(2)}) collective-permute-start(f32[20,64,128]{2,1,0:T(8,128)S(1)} %multiply_add_fusion.2), channel_id=1, source_target_pairs={{0,4},{4,8},{8,12},{12,16},{16,20},{20,24},{24,28},{28,32},{32,36}... | collective-permute-start | bytes 1966088 | tf_op jit(solution)/shard_map/while/body/eval_jaxpr/ppermute | solution.py:13
  513.4 15.3 %collective-permute-start = (f32[20,64,128]{2,1,0:T(8,128)S(1)}, f32[20,64,128]{2,1,0:T(8,128)S(1)}, u32[]{:S(2)}, u32[]{:S(2)}) collective-permute-start(f32[20,64,128]{2,1,0:T(8,128)S(1)} %multiply_add_fusion.2), channel_id=1, source_target_pairs={{0,4},{4,8},{8,12},{12,16},{16,20},{20,24},{24,28},{28,32},{32,36}... | collective-permute-start | bytes 1966088 | tf_op jit(solution)/shard_map/while/body/eval_jaxpr/ppermute | solution.py:13
  528.8 15.2 %collective-permute-start = (f32[20,64,128]{2,1,0:T(8,128)S(1)}, f32[20,64,128]{2,1,0:T(8,128)S(1)}, u32[]{:S(2)}, u32[]{:S(2)}) collective-permute-start(f32[20,64,128]{2,1,0:T(8,128)S(1)} %multiply_add_fusion.2), channel_id=1, source_target_pairs={{0,4},{4,8},{8,12},{12,16},{16,20},{20,24},{24,28},{28,32},{32,36}... | collective-permute-start | bytes 1966088 | tf_op jit(solution)/shard_map/while/body/eval_jaxpr/ppermute | solution.py:13
  544.1 16.3 %collective-permute-start = (f32[20,64,128]{2,1,0:T(8,128)S(1)}, f32[20,64,128]{2,1,0:T(8,128)S(1)}, u32[]{:S(2)}, u32[]{:S(2)}) collective-permute-start(f32[20,64,128]{2,1,0:T(8,128)S(1)} %multiply_add_fusion.2), channel_id=1, source_target_pairs={{0,4},{4,8},{8,12},{12,16},{16,20},{20,24},{24,28},{28,32},{32,36}... | collective-permute-start | bytes 1966088 | tf_op jit(solution)/shard_map/while/body/eval_jaxpr/ppermute | solution.py:13
  560.6 17.5 %collective-permute-start = (f32[20,64,128]{2,1,0:T(8,128)S(1)}, f32[20,64,128]{2,1,0:T(8,128)S(1)}, u32[]{:S(2)}, u32[]{:S(2)}) collective-permute-start(f32[20,64,128]{2,1,0:T(8,128)S(1)} %multiply_add_fusion.2), channel_id=1, source_target_pairs={{0,4},{4,8},{8,12},{12,16},{16,20},{20,24},{24,28},{28,32},{32,36}... | collective-permute-start | bytes 1966088 | tf_op jit(solution)/shard_map/while/body/eval_jaxpr/ppermute | solution.py:13
  578.2 18.6 %collective-permute-start = (f32[20,64,128]{2,1,0:T(8,128)S(1)}, f32[20,64,128]{2,1,0:T(8,128)S(1)}, u32[]{:S(2)}, u32[]{:S(2)}) collective-permute-start(f32[20,64,128]{2,1,0:T(8,128)S(1)} %multiply_add_fusion.2), channel_id=1, source_target_pairs={{0,4},{4,8},{8,12},{12,16},{16,20},{20,24},{24,28},{28,32},{32,36}... | collective-permute-start | bytes 1966088 | tf_op jit(solution)/shard_map/while/body/eval_jaxpr/ppermute | solution.py:13
  597.0 19.8 %collective-permute-start = (f32[20,64,128]{2,1,0:T(8,128)S(1)}, f32[20,64,128]{2,1,0:T(8,128)S(1)}, u32[]{:S(2)}, u32[]{:S(2)}) collective-permute-start(f32[20,64,128]{2,1,0:T(8,128)S(1)} %multiply_add_fusion.2), channel_id=1, source_target_pairs={{0,4},{4,8},{8,12},{12,16},{16,20},{20,24},{24,28},{28,32},{32,36}... | collective-permute-start | bytes 1966088 | tf_op jit(solution)/shard_map/while/body/eval_jaxpr/ppermute | solution.py:13
  616.9 20.9 %collective-permute-start = (f32[20,64,128]{2,1,0:T(8,128)S(1)}, f32[20,64,128]{2,1,0:T(8,128)S(1)}, u32[]{:S(2)}, u32[]{:S(2)}) collective-permute-start(f32[20,64,128]{2,1,0:T(8,128)S(1)} %multiply_add_fusion.2), channel_id=1, source_target_pairs={{0,4},{4,8},{8,12},{12,16},{16,20},{20,24},{24,28},{28,32},{32,36}... | collective-permute-start | bytes 1966088 | tf_op jit(solution)/shard_map/while/body/eval_jaxpr/ppermute | solution.py:13
  637.9 21.2 %collective-permute-start = (f32[20,64,128]{2,1,0:T(8,128)S(1)}, f32[20,64,128]{2,1,0:T(8,128)S(1)}, u32[]{:S(2)}, u32[]{:S(2)}) collective-permute-start(f32[20,64,128]{2,1,0:T(8,128)S(1)} %multiply_add_fusion.2), channel_id=1, source_target_pairs={{0,4},{4,8},{8,12},{12,16},{16,20},{20,24},{24,28},{28,32},{32,36}... | collective-permute-start | bytes 1966088 | tf_op jit(solution)/shard_map/while/body/eval_jaxpr/ppermute | solution.py:13
  659.2 20.3 %collective-permute-start = (f32[20,64,128]{2,1,0:T(8,128)S(1)}, f32[20,64,128]{2,1,0:T(8,128)S(1)}, u32[]{:S(2)}, u32[]{:S(2)}) collective-permute-start(f32[20,64,128]{2,1,0:T(8,128)S(1)} %multiply_add_fusion.2), channel_id=1, source_target_pairs={{0,4},{4,8},{8,12},{12,16},{16,20},{20,24},{24,28},{28,32},{32,36}... | collective-permute-start | bytes 1966088 | tf_op jit(solution)/shard_map/while/body/eval_jaxpr/ppermute | solution.py:13
  679.6 19.4 %collective-permute-start = (f32[20,64,128]{2,1,0:T(8,128)S(1)}, f32[20,64,128]{2,1,0:T(8,128)S(1)}, u32[]{:S(2)}, u32[]{:S(2)}) collective-permute-start(f32[20,64,128]{2,1,0:T(8,128)S(1)} %multiply_add_fusion.2), channel_id=1, source_target_pairs={{0,4},{4,8},{8,12},{12,16},{16,20},{20,24},{24,28},{28,32},{32,36}... | collective-permute-start | bytes 1966088 | tf_op jit(solution)/shard_map/while/body/eval_jaxpr/ppermute | solution.py:13
  699.2 18.6 %collective-permute-start = (f32[20,64,128]{2,1,0:T(8,128)S(1)}, f32[20,64,128]{2,1,0:T(8,128)S(1)}, u32[]{:S(2)}, u32[]{:S(2)}) collective-permute-start(f32[20,64,128]{2,1,0:T(8,128)S(1)} %multiply_add_fusion.2), channel_id=1, source_target_pairs={{0,4},{4,8},{8,12},{12,16},{16,20},{20,24},{24,28},{28,32},{32,36}... | collective-permute-start | bytes 1966088 | tf_op jit(solution)/shard_map/while/body/eval_jaxpr/ppermute | solution.py:13
  717.9 17.7 %collective-permute-start = (f32[20,64,128]{2,1,0:T(8,128)S(1)}, f32[20,64,128]{2,1,0:T(8,128)S(1)}, u32[]{:S(2)}, u32[]{:S(2)}) collective-permute-start(f32[20,64,128]{2,1,0:T(8,128)S(1)} %multiply_add_fusion.2), channel_id=1, source_target_pairs={{0,4},{4,8},{8,12},{12,16},{16,20},{20,24},{24,28},{28,32},{32,36}... | collective-permute-start | bytes 1966088 | tf_op jit(solution)/shard_map/while/body/eval_jaxpr/ppermute | solution.py:13
  735.8 16.9 %collective-permute-start = (f32[20,64,128]{2,1,0:T(8,128)S(1)}, f32[20,64,128]{2,1,0:T(8,128)S(1)}, u32[]{:S(2)}, u32[]{:S(2)}) collective-permute-start(f32[20,64,128]{2,1,0:T(8,128)S(1)} %multiply_add_fusion.2), channel_id=1, source_target_pairs={{0,4},{4,8},{8,12},{12,16},{16,20},{20,24},{24,28},{28,32},{32,36}... | collective-permute-start | bytes 1966088 | tf_op jit(solution)/shard_map/while/body/eval_jaxpr/ppermute | solution.py:13
  752.8 16.0 %collective-permute-start = (f32[20,64,128]{2,1,0:T(8,128)S(1)}, f32[20,64,128]{2,1,0:T(8,128)S(1)}, u32[]{:S(2)}, u32[]{:S(2)}) collective-permute-start(f32[20,64,128]{2,1,0:T(8,128)S(1)} %multiply_add_fusion.2), channel_id=1, source_target_pairs={{0,4},{4,8},{8,12},{12,16},{16,20},{20,24},{24,28},{28,32},{32,36}... | collective-permute-start | bytes 1966088 | tf_op jit(solution)/shard_map/while/body/eval_jaxpr/ppermute | solution.py:13
  769.0 15.2 %collective-permute-start = (f32[20,64,128]{2,1,0:T(8,128)S(1)}, f32[20,64,128]{2,1,0:T(8,128)S(1)}, u32[]{:S(2)}, u32[]{:S(2)}) collective-permute-start(f32[20,64,128]{2,1,0:T(8,128)S(1)} %multiply_add_fusion.2), channel_id=1, source_target_pairs={{0,4},{4,8},{8,12},{12,16},{16,20},{20,24},{24,28},{28,32},{32,36}... | collective-permute-start | bytes 1966088 | tf_op jit(solution)/shard_map/while/body/eval_jaxpr/ppermute | solution.py:13
  784.2 15.3 %collective-permute-start = (f32[20,64,128]{2,1,0:T(8,128)S(1)}, f32[20,64,128]{2,1,0:T(8,128)S(1)}, u32[]{:S(2)}, u32[]{:S(2)}) collective-permute-start(f32[20,64,128]{2,1,0:T(8,128)S(1)} %multiply_add_fusion.2), channel_id=1, source_target_pairs={{0,4},{4,8},{8,12},{12,16},{16,20},{20,24},{24,28},{28,32},{32,36}... | collective-permute-start | bytes 1966088 | tf_op jit(solution)/shard_map/while/body/eval_jaxpr/ppermute | solution.py:13
  799.7 16.5 %collective-permute-start = (f32[20,64,128]{2,1,0:T(8,128)S(1)}, f32[20,64,128]{2,1,0:T(8,128)S(1)}, u32[]{:S(2)}, u32[]{:S(2)}) collective-permute-start(f32[20,64,128]{2,1,0:T(8,128)S(1)} %multiply_add_fusion.2), channel_id=1, source_target_pairs={{0,4},{4,8},{8,12},{12,16},{16,20},{20,24},{24,28},{28,32},{32,36}... | collective-permute-start | bytes 1966088 | tf_op jit(solution)/shard_map/while/body/eval_jaxpr/ppermute | solution.py:13
  816.3 17.6 %collective-permute-start = (f32[20,64,128]{2,1,0:T(8,128)S(1)}, f32[20,64,128]{2,1,0:T(8,128)S(1)}, u32[]{:S(2)}, u32[]{:S(2)}) collective-permute-start(f32[20,64,128]{2,1,0:T(8,128)S(1)} %multiply_add_fusion.2), channel_id=1, source_target_pairs={{0,4},{4,8},{8,12},{12,16},{16,20},{20,24},{24,28},{28,32},{32,36}... | collective-permute-start | bytes 1966088 | tf_op jit(solution)/shard_map/while/body/eval_jaxpr/ppermute | solution.py:13
  834.1 18.8 %collective-permute-start = (f32[20,64,128]{2,1,0:T(8,128)S(1)}, f32[20,64,128]{2,1,0:T(8,128)S(1)}, u32[]{:S(2)}, u32[]{:S(2)}) collective-permute-start(f32[20,64,128]{2,1,0:T(8,128)S(1)} %multiply_add_fusion.2), channel_id=1, source_target_pairs={{0,4},{4,8},{8,12},{12,16},{16,20},{20,24},{24,28},{28,32},{32,36}... | collective-permute-start | bytes 1966088 | tf_op jit(solution)/shard_map/while/body/eval_jaxpr/ppermute | solution.py:13
  853.0 19.9 %collective-permute-start = (f32[20,64,128]{2,1,0:T(8,128)S(1)}, f32[20,64,128]{2,1,0:T(8,128)S(1)}, u32[]{:S(2)}, u32[]{:S(2)}) collective-permute-start(f32[20,64,128]{2,1,0:T(8,128)S(1)} %multiply_add_fusion.2), channel_id=1, source_target_pairs={{0,4},{4,8},{8,12},{12,16},{16,20},{20,24},{24,28},{28,32},{32,36}... | collective-permute-start | bytes 1966088 | tf_op jit(solution)/shard_map/while/body/eval_jaxpr/ppermute | solution.py:13
  873.1 21.1 %collective-permute-start = (f32[20,64,128]{2,1,0:T(8,128)S(1)}, f32[20,64,128]{2,1,0:T(8,128)S(1)}, u32[]{:S(2)}, u32[]{:S(2)}) collective-permute-start(f32[20,64,128]{2,1,0:T(8,128)S(1)} %multiply_add_fusion.2), channel_id=1, source_target_pairs={{0,4},{4,8},{8,12},{12,16},{16,20},{20,24},{24,28},{28,32},{32,36}... | collective-permute-start | bytes 1966088 | tf_op jit(solution)/shard_map/while/body/eval_jaxpr/ppermute | solution.py:13
  894.3 21.0 %collective-permute-start = (f32[20,64,128]{2,1,0:T(8,128)S(1)}, f32[20,64,128]{2,1,0:T(8,128)S(1)}, u32[]{:S(2)}, u32[]{:S(2)}) collective-permute-start(f32[20,64,128]{2,1,0:T(8,128)S(1)} %multiply_add_fusion.2), channel_id=1, source_target_pairs={{0,4},{4,8},{8,12},{12,16},{16,20},{20,24},{24,28},{28,32},{32,36}... | collective-permute-start | bytes 1966088 | tf_op jit(solution)/shard_map/while/body/eval_jaxpr/ppermute | solution.py:13
  915.4 20.1 %collective-permute-start = (f32[20,64,128]{2,1,0:T(8,128)S(1)}, f32[20,64,128]{2,1,0:T(8,128)S(1)}, u32[]{:S(2)}, u32[]{:S(2)}) collective-permute-start(f32[20,64,128]{2,1,0:T(8,128)S(1)} %multiply_add_fusion.2), channel_id=1, source_target_pairs={{0,4},{4,8},{8,12},{12,16},{16,20},{20,24},{24,28},{28,32},{32,36}... | collective-permute-start | bytes 1966088 | tf_op jit(solution)/shard_map/while/body/eval_jaxpr/ppermute | solution.py:13
  935.7 19.3 %collective-permute-start = (f32[20,64,128]{2,1,0:T(8,128)S(1)}, f32[20,64,128]{2,1,0:T(8,128)S(1)}, u32[]{:S(2)}, u32[]{:S(2)}) collective-permute-start(f32[20,64,128]{2,1,0:T(8,128)S(1)} %multiply_add_fusion.2), channel_id=1, source_target_pairs={{0,4},{4,8},{8,12},{12,16},{16,20},{20,24},{24,28},{28,32},{32,36}... | collective-permute-start | bytes 1966088 | tf_op jit(solution)/shard_map/while/body/eval_jaxpr/ppermute | solution.py:13
  955.1 18.4 %collective-permute-start = (f32[20,64,128]{2,1,0:T(8,128)S(1)}, f32[20,64,128]{2,1,0:T(8,128)S(1)}, u32[]{:S(2)}, u32[]{:S(2)}) collective-permute-start(f32[20,64,128]{2,1,0:T(8,128)S(1)} %multiply_add_fusion.2), channel_id=1, source_target_pairs={{0,4},{4,8},{8,12},{12,16},{16,20},{20,24},{24,28},{28,32},{32,36}... | collective-permute-start | bytes 1966088 | tf_op jit(solution)/shard_map/while/body/eval_jaxpr/ppermute | solution.py:13
  973.7 17.6 %collective-permute-start = (f32[20,64,128]{2,1,0:T(8,128)S(1)}, f32[20,64,128]{2,1,0:T(8,128)S(1)}, u32[]{:S(2)}, u32[]{:S(2)}) collective-permute-start(f32[20,64,128]{2,1,0:T(8,128)S(1)} %multiply_add_fusion.2), channel_id=1, source_target_pairs={{0,4},{4,8},{8,12},{12,16},{16,20},{20,24},{24,28},{28,32},{32,36}... | collective-permute-start | bytes 1966088 | tf_op jit(solution)/shard_map/while/body/eval_jaxpr/ppermute | solution.py:13
  991.4 14.6 %collective-permute-start = (f32[20,64,128]{2,1,0:T(8,128)S(1)}, f32[20,64,128]{2,1,0:T(8,128)S(1)}, u32[]{:S(2)}, u32[]{:S(2)}) collective-permute-start(f32[20,64,128]{2,1,0:T(8,128)S(1)} %multiply_add_fusion.2), channel_id=1, source_target_pairs={{0,4},{4,8},{8,12},{12,16},{16,20},{20,24},{24,28},{28,32},{32,36}... | collective-permute-start | bytes 1966088 | tf_op jit(solution)/shard_map/while/body/eval_jaxpr/ppermute | solution.py:13
  1006.1 14.6 %collective-permute-start = (f32[20,64,128]{2,1,0:T(8,128)S(1)}, f32[20,64,128]{2,1,0:T(8,128)S(1)}, u32[]{:S(2)}, u32[]{:S(2)}) collective-permute-start(f32[20,64,128]{2,1,0:T(8,128)S(1)} %multiply_add_fusion.2), channel_id=1, source_target_pairs={{0,4},{4,8},{8,12},{12,16},{16,20},{20,24},{24,28},{28,32},{32,36}... | collective-permute-start | bytes 1966088 | tf_op jit(solution)/shard_map/while/body/eval_jaxpr/ppermute | solution.py:13
  1020.7 4.2 copy-start
  1020.7 4.3 copy-start.6
Sparse Core Ops, SparseCore 0:
  26.1 36.3 all-gather.1
where the time goes:
time: 1110 us; the launch traced here: 1100 us
  waiting for transfers between devices  556 us (50%)
  local copies, waits for them, and re-layouts  324 us (29%)
  starting transfers between devices  73.4 us (7%)
  matrix products  49.4 us (4%)
  other arithmetic  43.6 us (4%)
  blocking collectives  36.9 us (3%)
  between operations  13.7 us (1%)
    ppermute x32, waiting for transfers between devices, from_behind(): return lax.ppermute(value, axis, pairs)  497 us
    dynamic_update_slice x16, local copies, waits for them, and re-layouts, per_device(): lax.scan(block_terms, start_state, (c_rows.reshape(block_count, SPAN, sta...  251 us
    ppermute x32, starting transfers between devices, from_behind(): return lax.ppermute(value, axis, pairs)  63.7 us
    all_to_all x1, blocking collectives, per_device(): lax.all_to_all(regrouped, 'head', split_axis=0, concat_axis=1, tiled=True)  36.9 us
    all_gather x1, waiting for transfers between devices, per_device(): state_whole = lax.all_gather(state_inputs, 'head', axis=0, tiled=True)  30.6 us
    all_to_all x1, waiting for transfers between devices, per_device(): lax.all_to_all(inner_tokens, 'head', split_axis=1, concat_axis=0, tiled=T...  26.9 us
  transfers between devices with their start and end apart: 35, of which 35 were waited for; matrix products, arithmetic and copies ran while one was open for 2% of the time, Pallas kernels for 0%

commit v1 on v0

--- a/solution.py
+++ b/solution.py
@@ -59,7 +59,9 @@
     heads_local = head_rates.shape[1]
     head_width = channels // heads_local
     margin_rows = KERNEL - 1
-    state_whole = lax.all_gather(state_inputs, "head", axis=0, tiled=True)
+    state_whole = jnp.concatenate(
+        lax.all_to_all(jnp.stack([state_inputs] * lax.axis_size("head")), "head", 0, 0), axis=0
+    )
     edge_rows = jnp.concatenate(
         [x_local[context - margin_rows :], state_whole[context - margin_rows :]], axis=1
     )

time: 1110 us -> 1100 us (level)
  between operations: 13.7 us -> 0.31 us
    all_gather x1 -> x0, waiting for transfers between devices: 30.6 us -> none  [per_device(): state_whole = lax.all_gather(state_inputs, 'head', axis=0, tiled=True)]
    all_to_all x1, waiting for transfers between devices: 26.9 us -> 49 us  [per_device(): lax.all_to_all(inner_tokens, 'head', split_axis=1, concat_axis=0, tiled=T...]
  transfers between devices with their start and end apart: 35 -> 34, of which waited for: 35 -> 34; matrix products, arithmetic and copies ran while one was open for 2% -> 2% of each run, Pallas kernels for 0% -> 0%
where the time goes in v1:
time: 1100 us; the launch traced here: 1090 us
  waiting for transfers between devices  553 us (50%)
  local copies, waits for them, and re-layouts  325 us (30%)
  starting transfers between devices  72.4 us (7%)
  matrix products  49.4 us (4%)
  blocking collectives  46.9 us (4%)
  other arithmetic  43.6 us (4%)
    ppermute x32, waiting for transfers between devices, from_behind(): return lax.ppermute(value, axis, pairs)  496 us
    dynamic_update_slice x16, local copies, waits for them, and re-layouts, per_device(): lax.scan(block_terms, start_state, (c_rows.reshape(block_count, SPAN, sta...  251 us
    ppermute x32, starting transfers between devices, from_behind(): return lax.ppermute(value, axis, pairs)  63.7 us
    all_to_all x1, waiting for transfers between devices, per_device(): lax.all_to_all(inner_tokens, 'head', split_axis=1, concat_axis=0, tiled=T...  49 us
    all_to_all x1, blocking collectives, per_device(): lax.all_to_all(regrouped, 'head', split_axis=0, concat_axis=1, tiled=True)  36.9 us
  transfers between devices with their start and end apart: 34, of which 34 were waited for; matrix products, arithmetic and copies ran while one was open for 2% of the time, Pallas kernels for 0%

profile of v1, /device:TPU:6, one launch (start us, length us, event | category | flops | bytes accessed | tf_op | source)
XLA Modules:
  0.0 1092.2 jit_solution(9254635637333386807)
XLA Ops:
  0.9 10.1 all_to_all.56
  44.7 49.0 %all-to-all-done.1 = bf16[512,4,1280]{2,0,1:T(8,128)(2,1)} async-done(((bf16[512,4,1280]{2,0,1:T(8,128)(2,1)}), bf16[512,4,1280]{2,0,1:T(8,128)(2,1)}, u32[]{:S(2)}, u32[]{:S(2)}) %all-to-all-start.1) | async-done | bytes 5242912 | tf_op jit(solution)/shard_map/all_to_all | solution.py:54
  112.4 11.4 %copy.83 = f32[2048,1280]{0,1:T(8,128)} copy(f32[2048,1280]{1,0:T(8,128)} %fusion.47) | data formatting | bytes 20971520 | tf_op jit(solution)/shard_map/convert_element_type | solution.py:78
  123.8 9.2 copy.101
  145.1 307.2 %while.24 = (s32[]{:T(128)}, f32[20,64,128]{2,1,0:T(8,128)S(1)}, f32[8,256,20,64]{1,0,3,2:T(8,128)}, f32[8,256,20]{1,0,2:T(8,128)S(1)}, bf16[8,256,20,64]{1,3,2,...) while((s32[]{:T(128)}, f32[20,64,128]{2,1,0:T(8,128)S(1)}, ...), condition=%wide.region_3.4_spmd.clone, body=%wide.region_0.3_spmd.clone.sunk | while | flops 1199117312 | bytes 13914835 | solution.py:81
  153.7 30.0 %dynamic_update_slice.6 = f32[8,256,20,64]{1,0,3,2:T(8,128)} dynamic-update-slice(f32[8,256,20,64]{1,0,3,2:T(8,128)} %get-tuple-element.251, f32[1,256,20,64]{1,0,3,2:T(1,128)S(1)} %copy.120, s32[]{:T(128)S(6)} %copy.125, s32[]{:T(128)} %constant.36.clone.1..sunk, s32[]{:T(128)} %constant.36.clone.1..sunk, s32[]{:T(128)} %constant.36.clone.1..sunk) | dynamic-update-slice | bytes 2621444 | tf_op jit(solution)/shard_map/while/body/jit(dynamic_update_index_in_dim)/dynamic_update_slice | solution.py:81
  192.1 30.0 %dynamic_update_slice.6 = f32[8,256,20,64]{1,0,3,2:T(8,128)} dynamic-update-slice(f32[8,256,20,64]{1,0,3,2:T(8,128)} %get-tuple-element.251, f32[1,256,20,64]{1,0,3,2:T(1,128)S(1)} %copy.120, s32[]{:T(128)S(6)} %copy.125, s32[]{:T(128)} %constant.36.clone.1..sunk, s32[]{:T(128)} %constant.36.clone.1..sunk, s32[]{:T(128)} %constant.36.clone.1..sunk) | dynamic-update-slice | bytes 2621444 | tf_op jit(solution)/shard_map/while/body/jit(dynamic_update_index_in_dim)/dynamic_update_slice | solution.py:81
  230.5 30.0 %dynamic_update_slice.6 = f32[8,256,20,64]{1,0,3,2:T(8,128)} dynamic-update-slice(f32[8,256,20,64]{1,0,3,2:T(8,128)} %get-tuple-element.251, f32[1,256,20,64]{1,0,3,2:T(1,128)S(1)} %copy.120, s32[]{:T(128)S(6)} %copy.125, s32[]{:T(128)} %constant.36.clone.1..sunk, s32[]{:T(128)} %constant.36.clone.1..sunk, s32[]{:T(128)} %constant.36.clone.1..sunk) | dynamic-update-slice | bytes 2621444 | tf_op jit(solution)/shard_map/while/body/jit(dynamic_update_index_in_dim)/dynamic_update_slice | solution.py:81
  268.8 30.0 %dynamic_update_slice.6 = f32[8,256,20,64]{1,0,3,2:T(8,128)} dynamic-update-slice(f32[8,256,20,64]{1,0,3,2:T(8,128)} %get-tuple-element.251, f32[1,256,20,64]{1,0,3,2:T(1,128)S(1)} %copy.120, s32[]{:T(128)S(6)} %copy.125, s32[]{:T(128)} %constant.36.clone.1..sunk, s32[]{:T(128)} %constant.36.clone.1..sunk, s32[]{:T(128)} %constant.36.clone.1..sunk) | dynamic-update-slice | bytes 2621444 | tf_op jit(solution)/shard_map/while/body/jit(dynamic_update_index_in_dim)/dynamic_update_slice | solution.py:81
  307.2 30.0 %dynamic_update_slice.6 = f32[8,256,20,64]{1,0,3,2:T(8,128)} dynamic-update-slice(f32[8,256,20,64]{1,0,3,2:T(8,128)} %get-tuple-element.251, f32[1,256,20,64]{1,0,3,2:T(1,128)S(1)} %copy.120, s32[]{:T(128)S(6)} %copy.125, s32[]{:T(128)} %constant.36.clone.1..sunk, s32[]{:T(128)} %constant.36.clone.1..sunk, s32[]{:T(128)} %constant.36.clone.1..sunk) | dynamic-update-slice | bytes 2621444 | tf_op jit(solution)/shard_map/while/body/jit(dynamic_update_index_in_dim)/dynamic_update_slice | solution.py:81
  345.6 30.0 %dynamic_update_slice.6 = f32[8,256,20,64]{1,0,3,2:T(8,128)} dynamic-update-slice(f32[8,256,20,64]{1,0,3,2:T(8,128)} %get-tuple-element.251, f32[1,256,20,64]{1,0,3,2:T(1,128)S(1)} %copy.120, s32[]{:T(128)S(6)} %copy.125, s32[]{:T(128)} %constant.36.clone.1..sunk, s32[]{:T(128)} %constant.36.clone.1..sunk, s32[]{:T(128)} %constant.36.clone.1..sunk) | dynamic-update-slice | bytes 2621444 | tf_op jit(solution)/shard_map/while/body/jit(dynamic_update_index_in_dim)/dynamic_update_slice | solution.py:81
  383.9 30.0 %dynamic_update_slice.6 = f32[8,256,20,64]{1,0,3,2:T(8,128)} dynamic-update-slice(f32[8,256,20,64]{1,0,3,2:T(8,128)} %get-tuple-element.251, f32[1,256,20,64]{1,0,3,2:T(1,128)S(1)} %copy.120, s32[]{:T(128)S(6)} %copy.125, s32[]{:T(128)} %constant.36.clone.1..sunk, s32[]{:T(128)} %constant.36.clone.1..sunk, s32[]{:T(128)} %constant.36.clone.1..sunk) | dynamic-update-slice | bytes 2621444 | tf_op jit(solution)/shard_map/while/body/jit(dynamic_update_index_in_dim)/dynamic_update_slice | solution.py:81
  422.3 30.0 %dynamic_update_slice.6 = f32[8,256,20,64]{1,0,3,2:T(8,128)} dynamic-update-slice(f32[8,256,20,64]{1,0,3,2:T(8,128)} %get-tuple-element.251, f32[1,256,20,64]{1,0,3,2:T(1,128)S(1)} %copy.120, s32[]{:T(128)S(6)} %copy.125, s32[]{:T(128)} %constant.36.clone.1..sunk, s32[]{:T(128)} %constant.36.clone.1..sunk, s32[]{:T(128)} %constant.36.clone.1..sunk) | dynamic-update-slice | bytes 2621444 | tf_op jit(solution)/shard_map/while/body/jit(dynamic_update_index_in_dim)/dynamic_update_slice | solution.py:81
  452.3 11.4 %reshape.146 = f32[2048,20,64]{0,2,1:T(8,128)} reshape(f32[8,256,20,64]{1,0,3,2:T(8,128)} %get-tuple-element.65) | data formatting | bytes 20971520 | tf_op jit(solution)/shard_map/reshape | solution.py:102
  463.8 557.4 %while.23 = (s32[]{:T(128)}, f32[20,64,128]{2,1,0:T(8,128)S(1)}, f32[20]{0:T(128)S(1)}, f32[20,64,128]{2,1,0:T(8,128)S(1)}, s32[]{:T(128)}) while((s32[]{:T(128)}, f32[20,64,128]{2,1,0:T(8,128)S(1)}, f32[20]{0:T(128)S(1)}, f32[20,64,128]{2,1,0:T(8,128)S(1)}, s32[]{:T(128)}) %tuple.57), condition=%wide.region_7.8_spmd, body=%wide.region_6.7_spmd.sunk | while | flops 327682 | bytes 4587701 | solution.py:97
  466.1 14.5 %collective-permute-done = f32[20,64,128]{2,1,0:T(8,128)S(1)} collective-permute-done((f32[20,64,128]{2,1,0:T(8,128)S(1)}, f32[20,64,128]{2,1,0:T(8,128)S(1)}, u32[]{:S(2)}, u32[]{:S(2)}) %collective-permute-start) | collective-permute-done | bytes 655392 | tf_op jit(solution)/shard_map/while/body/eval_jaxpr/ppermute | solution.py:13
  482.6 13.7 %collective-permute-done = f32[20,64,128]{2,1,0:T(8,128)S(1)} collective-permute-done((f32[20,64,128]{2,1,0:T(8,128)S(1)}, f32[20,64,128]{2,1,0:T(8,128)S(1)}, u32[]{:S(2)}, u32[]{:S(2)}) %collective-permute-start) | collective-permute-done | bytes 655392 | tf_op jit(solution)/shard_map/while/body/eval_jaxpr/ppermute | solution.py:13
  498.4 12.8 %collective-permute-done = f32[20,64,128]{2,1,0:T(8,128)S(1)} collective-permute-done((f32[20,64,128]{2,1,0:T(8,128)S(1)}, f32[20,64,128]{2,1,0:T(8,128)S(1)}, u32[]{:S(2)}, u32[]{:S(2)}) %collective-permute-start) | collective-permute-done | bytes 655392 | tf_op jit(solution)/shard_map/while/body/eval_jaxpr/ppermute | solution.py:13
  513.3 13.8 %collective-permute-done = f32[20,64,128]{2,1,0:T(8,128)S(1)} collective-permute-done((f32[20,64,128]{2,1,0:T(8,128)S(1)}, f32[20,64,128]{2,1,0:T(8,128)S(1)}, u32[]{:S(2)}, u32[]{:S(2)}) %collective-permute-start) | collective-permute-done | bytes 655392 | tf_op jit(solution)/shard_map/while/body/eval_jaxpr/ppermute | solution.py:13
  529.2 15.0 %collective-permute-done = f32[20,64,128]{2,1,0:T(8,128)S(1)} collective-permute-done((f32[20,64,128]{2,1,0:T(8,128)S(1)}, f32[20,64,128]{2,1,0:T(8,128)S(1)}, u32[]{:S(2)}, u32[]{:S(2)}) %collective-permute-start) | collective-permute-done | bytes 655392 | tf_op jit(solution)/shard_map/while/body/eval_jaxpr/ppermute | solution.py:13
  546.2 16.1 %collective-permute-done = f32[20,64,128]{2,1,0:T(8,128)S(1)} collective-permute-done((f32[20,64,128]{2,1,0:T(8,128)S(1)}, f32[20,64,128]{2,1,0:T(8,128)S(1)}, u32[]{:S(2)}, u32[]{:S(2)}) %collective-permute-start) | collective-permute-done | bytes 655392 | tf_op jit(solution)/shard_map/while/body/eval_jaxpr/ppermute | solution.py:13
  564.4 17.3 %collective-permute-done = f32[20,64,128]{2,1,0:T(8,128)S(1)} collective-permute-done((f32[20,64,128]{2,1,0:T(8,128)S(1)}, f32[20,64,128]{2,1,0:T(8,128)S(1)}, u32[]{:S(2)}, u32[]{:S(2)}) %collective-permute-start) | collective-permute-done | bytes 655392 | tf_op jit(solution)/shard_map/while/body/eval_jaxpr/ppermute | solution.py:13
  583.7 18.4 %collective-permute-done = f32[20,64,128]{2,1,0:T(8,128)S(1)} collective-permute-done((f32[20,64,128]{2,1,0:T(8,128)S(1)}, f32[20,64,128]{2,1,0:T(8,128)S(1)}, u32[]{:S(2)}, u32[]{:S(2)}) %collective-permute-start) | collective-permute-done | bytes 655392 | tf_op jit(solution)/shard_map/while/body/eval_jaxpr/ppermute | solution.py:13
  604.2 19.6 %collective-permute-done = f32[20,64,128]{2,1,0:T(8,128)S(1)} collective-permute-done((f32[20,64,128]{2,1,0:T(8,128)S(1)}, f32[20,64,128]{2,1,0:T(8,128)S(1)}, u32[]{:S(2)}, u32[]{:S(2)}) %collective-permute-start) | collective-permute-done | bytes 655392 | tf_op jit(solution)/shard_map/while/body/eval_jaxpr/ppermute | solution.py:13
  625.8 18.8 %collective-permute-done = f32[20,64,128]{2,1,0:T(8,128)S(1)} collective-permute-done((f32[20,64,128]{2,1,0:T(8,128)S(1)}, f32[20,64,128]{2,1,0:T(8,128)S(1)}, u32[]{:S(2)}, u32[]{:S(2)}) %collective-permute-start) | collective-permute-done | bytes 655392 | tf_op jit(solution)/shard_map/while/body/eval_jaxpr/ppermute | solution.py:13
  646.7 18.0 %collective-permute-done = f32[20,64,128]{2,1,0:T(8,128)S(1)} collective-permute-done((f32[20,64,128]{2,1,0:T(8,128)S(1)}, f32[20,64,128]{2,1,0:T(8,128)S(1)}, u32[]{:S(2)}, u32[]{:S(2)}) %collective-permute-start) | collective-permute-done | bytes 655392 | tf_op jit(solution)/shard_map/while/body/eval_jaxpr/ppermute | solution.py:13
  666.7 17.1 %collective-permute-done = f32[20,64,128]{2,1,0:T(8,128)S(1)} collective-permute-done((f32[20,64,128]{2,1,0:T(8,128)S(1)}, f32[20,64,128]{2,1,0:T(8,128)S(1)}, u32[]{:S(2)}, u32[]{:S(2)}) %collective-permute-start) | collective-permute-done | bytes 655392 | tf_op jit(solution)/shard_map/while/body/eval_jaxpr/ppermute | solution.py:13
  685.9 16.3 %collective-permute-done = f32[20,64,128]{2,1,0:T(8,128)S(1)} collective-permute-done((f32[20,64,128]{2,1,0:T(8,128)S(1)}, f32[20,64,128]{2,1,0:T(8,128)S(1)}, u32[]{:S(2)}, u32[]{:S(2)}) %collective-permute-start) | collective-permute-done | bytes 655392 | tf_op jit(solution)/shard_map/while/body/eval_jaxpr/ppermute | solution.py:13
  704.2 15.4 %collective-permute-done = f32[20,64,128]{2,1,0:T(8,128)S(1)} collective-permute-done((f32[20,64,128]{2,1,0:T(8,128)S(1)}, f32[20,64,128]{2,1,0:T(8,128)S(1)}, u32[]{:S(2)}, u32[]{:S(2)}) %collective-permute-start) | collective-permute-done | bytes 655392 | tf_op jit(solution)/shard_map/while/body/eval_jaxpr/ppermute | solution.py:13
  721.7 14.5 %collective-permute-done = f32[20,64,128]{2,1,0:T(8,128)S(1)} collective-permute-done((f32[20,64,128]{2,1,0:T(8,128)S(1)}, f32[20,64,128]{2,1,0:T(8,128)S(1)}, u32[]{:S(2)}, u32[]{:S(2)}) %collective-permute-start) | collective-permute-done | bytes 655392 | tf_op jit(solution)/shard_map/while/body/eval_jaxpr/ppermute | solution.py:13
  738.3 13.7 %collective-permute-done = f32[20,64,128]{2,1,0:T(8,128)S(1)} collective-permute-done((f32[20,64,128]{2,1,0:T(8,128)S(1)}, f32[20,64,128]{2,1,0:T(8,128)S(1)}, u32[]{:S(2)}, u32[]{:S(2)}) %collective-permute-start) | collective-permute-done | bytes 655392 | tf_op jit(solution)/shard_map/while/body/eval_jaxpr/ppermute | solution.py:13
  754.0 12.8 %collective-permute-done = f32[20,64,128]{2,1,0:T(8,128)S(1)} collective-permute-done((f32[20,64,128]{2,1,0:T(8,128)S(1)}, f32[20,64,128]{2,1,0:T(8,128)S(1)}, u32[]{:S(2)}, u32[]{:S(2)}) %collective-permute-start) | collective-permute-done | bytes 655392 | tf_op jit(solution)/shard_map/while/body/eval_jaxpr/ppermute | solution.py:13
  768.9 13.8 %collective-permute-done = f32[20,64,128]{2,1,0:T(8,128)S(1)} collective-permute-done((f32[20,64,128]{2,1,0:T(8,128)S(1)}, f32[20,64,128]{2,1,0:T(8,128)S(1)}, u32[]{:S(2)}, u32[]{:S(2)}) %collective-permute-start) | collective-permute-done | bytes 655392 | tf_op jit(solution)/shard_map/while/body/eval_jaxpr/ppermute | solution.py:13
  784.8 14.9 %collective-permute-done = f32[20,64,128]{2,1,0:T(8,128)S(1)} collective-permute-done((f32[20,64,128]{2,1,0:T(8,128)S(1)}, f32[20,64,128]{2,1,0:T(8,128)S(1)}, u32[]{:S(2)}, u32[]{:S(2)}) %collective-permute-start) | collective-permute-done | bytes 655392 | tf_op jit(solution)/shard_map/while/body/eval_jaxpr/ppermute | solution.py:13
  801.8 16.1 %collective-permute-done = f32[20,64,128]{2,1,0:T(8,128)S(1)} collective-permute-done((f32[20,64,128]{2,1,0:T(8,128)S(1)}, f32[20,64,128]{2,1,0:T(8,128)S(1)}, u32[]{:S(2)}, u32[]{:S(2)}) %collective-permute-start) | collective-permute-done | bytes 655392 | tf_op jit(solution)/shard_map/while/body/eval_jaxpr/ppermute | solution.py:13
  820.0 17.2 %collective-permute-done = f32[20,64,128]{2,1,0:T(8,128)S(1)} collective-permute-done((f32[20,64,128]{2,1,0:T(8,128)S(1)}, f32[20,64,128]{2,1,0:T(8,128)S(1)}, u32[]{:S(2)}, u32[]{:S(2)}) %collective-permute-start) | collective-permute-done | bytes 655392 | tf_op jit(solution)/shard_map/while/body/eval_jaxpr/ppermute | solution.py:13
  839.3 18.4 %collective-permute-done = f32[20,64,128]{2,1,0:T(8,128)S(1)} collective-permute-done((f32[20,64,128]{2,1,0:T(8,128)S(1)}, f32[20,64,128]{2,1,0:T(8,128)S(1)}, u32[]{:S(2)}, u32[]{:S(2)}) %collective-permute-start) | collective-permute-done | bytes 655392 | tf_op jit(solution)/shard_map/while/body/eval_jaxpr/ppermute | solution.py:13
  859.8 19.5 %collective-permute-done = f32[20,64,128]{2,1,0:T(8,128)S(1)} collective-permute-done((f32[20,64,128]{2,1,0:T(8,128)S(1)}, f32[20,64,128]{2,1,0:T(8,128)S(1)}, u32[]{:S(2)}, u32[]{:S(2)}) %collective-permute-start) | collective-permute-done | bytes 655392 | tf_op jit(solution)/shard_map/while/body/eval_jaxpr/ppermute | solution.py:13
  881.4 18.8 %collective-permute-done = f32[20,64,128]{2,1,0:T(8,128)S(1)} collective-permute-done((f32[20,64,128]{2,1,0:T(8,128)S(1)}, f32[20,64,128]{2,1,0:T(8,128)S(1)}, u32[]{:S(2)}, u32[]{:S(2)}) %collective-permute-start) | collective-permute-done | bytes 655392 | tf_op jit(solution)/shard_map/while/body/eval_jaxpr/ppermute | solution.py:13
  902.3 18.0 %collective-permute-done = f32[20,64,128]{2,1,0:T(8,128)S(1)} collective-permute-done((f32[20,64,128]{2,1,0:T(8,128)S(1)}, f32[20,64,128]{2,1,0:T(8,128)S(1)}, u32[]{:S(2)}, u32[]{:S(2)}) %collective-permute-start) | collective-permute-done | bytes 655392 | tf_op jit(solution)/shard_map/while/body/eval_jaxpr/ppermute | solution.py:13
  922.3 17.1 %collective-permute-done = f32[20,64,128]{2,1,0:T(8,128)S(1)} collective-permute-done((f32[20,64,128]{2,1,0:T(8,128)S(1)}, f32[20,64,128]{2,1,0:T(8,128)S(1)}, u32[]{:S(2)}, u32[]{:S(2)}) %collective-permute-start) | collective-permute-done | bytes 655392 | tf_op jit(solution)/shard_map/while/body/eval_jaxpr/ppermute | solution.py:13
  941.5 16.3 %collective-permute-done = f32[20,64,128]{2,1,0:T(8,128)S(1)} collective-permute-done((f32[20,64,128]{2,1,0:T(8,128)S(1)}, f32[20,64,128]{2,1,0:T(8,128)S(1)}, u32[]{:S(2)}, u32[]{:S(2)}) %collective-permute-start) | collective-permute-done | bytes 655392 | tf_op jit(solution)/shard_map/while/body/eval_jaxpr/ppermute | solution.py:13
  959.8 15.4 %collective-permute-done = f32[20,64,128]{2,1,0:T(8,128)S(1)} collective-permute-done((f32[20,64,128]{2,1,0:T(8,128)S(1)}, f32[20,64,128]{2,1,0:T(8,128)S(1)}, u32[]{:S(2)}, u32[]{:S(2)}) %collective-permute-start) | collective-permute-done | bytes 655392 | tf_op jit(solution)/shard_map/while/body/eval_jaxpr/ppermute | solution.py:13
  977.3 14.5 %collective-permute-done = f32[20,64,128]{2,1,0:T(8,128)S(1)} collective-permute-done((f32[20,64,128]{2,1,0:T(8,128)S(1)}, f32[20,64,128]{2,1,0:T(8,128)S(1)}, u32[]{:S(2)}, u32[]{:S(2)}) %collective-permute-start) | collective-permute-done | bytes 655392 | tf_op jit(solution)/shard_map/while/body/eval_jaxpr/ppermute | solution.py:13
  993.9 12.7 %collective-permute-done = f32[20,64,128]{2,1,0:T(8,128)S(1)} collective-permute-done((f32[20,64,128]{2,1,0:T(8,128)S(1)}, f32[20,64,128]{2,1,0:T(8,128)S(1)}, u32[]{:S(2)}, u32[]{:S(2)}) %collective-permute-start) | collective-permute-done | bytes 655392 | tf_op jit(solution)/shard_map/while/body/eval_jaxpr/ppermute | solution.py:13
  1008.6 12.7 %collective-permute-done = f32[20,64,128]{2,1,0:T(8,128)S(1)} collective-permute-done((f32[20,64,128]{2,1,0:T(8,128)S(1)}, f32[20,64,128]{2,1,0:T(8,128)S(1)}, u32[]{:S(2)}, u32[]{:S(2)}) %collective-permute-start) | collective-permute-done | bytes 655392 | tf_op jit(solution)/shard_map/while/body/eval_jaxpr/ppermute | solution.py:13
  1034.4 9.5 all_to_all.48
  1047.4 36.9 %all_to_all.57 = bf16[4,512,1280]{1,2,0:T(8,128)(2,1)} all-to-all(bf16[4,512,1280]{1,2,0:T(8,128)(2,1)S(1)} %copy.91), channel_id=1, replica_groups=mesh['run'=2,'ctx'=32,'head'=4] {'head'}, dimensions={0} | all-to-all | bytes 10485760 | tf_op jit(solution)/shard_map/all_to_all | solution.py:107
  (295 shorter events, 219.3 us)
Async XLA Ops:
  13.0 17.4 %all-to-all-start.2 = ((bf16[4,512,256]{2,1,0:T(8,128)(2,1)}), bf16[4,512,256]{2,1,0:T(8,128)(2,1)S(1)}, u32[]{:S(2)}, u32[]{:S(2)}) async-start(bf16[4,512,256]{2,1,0:T(8,128)(2,1)} %stack.2), calls=%async_computation.2 | async-start | bytes 2097152 | tf_op jit(solution)/shard_map/all_to_all | solution.py:63
  30.4 12.9 %copy-start.3 = (bf16[4,512,256]{2,1,0:T(8,128)(2,1)}, bf16[4,512,256]{2,1,0:T(8,128)(2,1)S(1)}, u32[]{:S(2)}) copy-start(bf16[4,512,256]{2,1,0:T(8,128)(2,1)S(1)} %all-to-all-done.2) | copy-start | bytes 3145732
  30.4 5.2 copy-start.4
  30.4 5.3 copy-start.6
  30.4 5.3 copy-start.5
  30.4 63.3 %all-to-all-start.1 = ((bf16[512,4,1280]{2,0,1:T(8,128)(2,1)}), bf16[512,4,1280]{2,0,1:T(8,128)(2,1)}, u32[]{:S(2)}, u32[]{:S(2)}) async-start(bf16[512,4,1280]{2,0,1:T(8,128)(2,1)} %bitcast.131), calls=%async_computation.1 | async-start | bytes 10485760 | tf_op jit(solution)/shard_map/all_to_all | solution.py:54
  94.5 9.7 collective-permute-start.1
  144.1 1.0 copy-start.1
  463.8 557.5 %copy-start.2 = (bf16[2048,256]{1,0:T(8,128)(2,1)S(1)}, bf16[2048,256]{1,0:T(8,128)(2,1)}, u32[]{:S(2)}) copy-start(bf16[2048,256]{1,0:T(8,128)(2,1)} %copy-done.1) | copy-start | bytes 3145732
  464.0 16.6 %collective-permute-start = (f32[20,64,128]{2,1,0:T(8,128)S(1)}, f32[20,64,128]{2,1,0:T(8,128)S(1)}, u32[]{:S(2)}, u32[]{:S(2)}) collective-permute-start(f32[20,64,128]{2,1,0:T(8,128)S(1)} %multiply_add_fusion.2), channel_id=1, source_target_pairs={{0,4},{4,8},{8,12},{12,16},{16,20},{20,24},{24,28},{28,32},{32,36}... | collective-permute-start | bytes 1966088 | tf_op jit(solution)/shard_map/while/body/eval_jaxpr/ppermute | solution.py:13
  480.7 15.6 %collective-permute-start = (f32[20,64,128]{2,1,0:T(8,128)S(1)}, f32[20,64,128]{2,1,0:T(8,128)S(1)}, u32[]{:S(2)}, u32[]{:S(2)}) collective-permute-start(f32[20,64,128]{2,1,0:T(8,128)S(1)} %multiply_add_fusion.2), channel_id=1, source_target_pairs={{0,4},{4,8},{8,12},{12,16},{16,20},{20,24},{24,28},{28,32},{32,36}... | collective-permute-start | bytes 1966088 | tf_op jit(solution)/shard_map/while/body/eval_jaxpr/ppermute | solution.py:13
  496.5 14.8 %collective-permute-start = (f32[20,64,128]{2,1,0:T(8,128)S(1)}, f32[20,64,128]{2,1,0:T(8,128)S(1)}, u32[]{:S(2)}, u32[]{:S(2)}) collective-permute-start(f32[20,64,128]{2,1,0:T(8,128)S(1)} %multiply_add_fusion.2), channel_id=1, source_target_pairs={{0,4},{4,8},{8,12},{12,16},{16,20},{20,24},{24,28},{28,32},{32,36}... | collective-permute-start | bytes 1966088 | tf_op jit(solution)/shard_map/while/body/eval_jaxpr/ppermute | solution.py:13
  511.4 15.8 %collective-permute-start = (f32[20,64,128]{2,1,0:T(8,128)S(1)}, f32[20,64,128]{2,1,0:T(8,128)S(1)}, u32[]{:S(2)}, u32[]{:S(2)}) collective-permute-start(f32[20,64,128]{2,1,0:T(8,128)S(1)} %multiply_add_fusion.2), channel_id=1, source_target_pairs={{0,4},{4,8},{8,12},{12,16},{16,20},{20,24},{24,28},{28,32},{32,36}... | collective-permute-start | bytes 1966088 | tf_op jit(solution)/shard_map/while/body/eval_jaxpr/ppermute | solution.py:13
  527.2 16.9 %collective-permute-start = (f32[20,64,128]{2,1,0:T(8,128)S(1)}, f32[20,64,128]{2,1,0:T(8,128)S(1)}, u32[]{:S(2)}, u32[]{:S(2)}) collective-permute-start(f32[20,64,128]{2,1,0:T(8,128)S(1)} %multiply_add_fusion.2), channel_id=1, source_target_pairs={{0,4},{4,8},{8,12},{12,16},{16,20},{20,24},{24,28},{28,32},{32,36}... | collective-permute-start | bytes 1966088 | tf_op jit(solution)/shard_map/while/body/eval_jaxpr/ppermute | solution.py:13
  544.3 18.0 %collective-permute-start = (f32[20,64,128]{2,1,0:T(8,128)S(1)}, f32[20,64,128]{2,1,0:T(8,128)S(1)}, u32[]{:S(2)}, u32[]{:S(2)}) collective-permute-start(f32[20,64,128]{2,1,0:T(8,128)S(1)} %multiply_add_fusion.2), channel_id=1, source_target_pairs={{0,4},{4,8},{8,12},{12,16},{16,20},{20,24},{24,28},{28,32},{32,36}... | collective-permute-start | bytes 1966088 | tf_op jit(solution)/shard_map/while/body/eval_jaxpr/ppermute | solution.py:13
  562.4 19.2 %collective-permute-start = (f32[20,64,128]{2,1,0:T(8,128)S(1)}, f32[20,64,128]{2,1,0:T(8,128)S(1)}, u32[]{:S(2)}, u32[]{:S(2)}) collective-permute-start(f32[20,64,128]{2,1,0:T(8,128)S(1)} %multiply_add_fusion.2), channel_id=1, source_target_pairs={{0,4},{4,8},{8,12},{12,16},{16,20},{20,24},{24,28},{28,32},{32,36}... | collective-permute-start | bytes 1966088 | tf_op jit(solution)/shard_map/while/body/eval_jaxpr/ppermute | solution.py:13
  581.8 20.3 %collective-permute-start = (f32[20,64,128]{2,1,0:T(8,128)S(1)}, f32[20,64,128]{2,1,0:T(8,128)S(1)}, u32[]{:S(2)}, u32[]{:S(2)}) collective-permute-start(f32[20,64,128]{2,1,0:T(8,128)S(1)} %multiply_add_fusion.2), channel_id=1, source_target_pairs={{0,4},{4,8},{8,12},{12,16},{16,20},{20,24},{24,28},{28,32},{32,36}... | collective-permute-start | bytes 1966088 | tf_op jit(solution)/shard_map/while/body/eval_jaxpr/ppermute | solution.py:13
  602.2 21.5 %collective-permute-start = (f32[20,64,128]{2,1,0:T(8,128)S(1)}, f32[20,64,128]{2,1,0:T(8,128)S(1)}, u32[]{:S(2)}, u32[]{:S(2)}) collective-permute-start(f32[20,64,128]{2,1,0:T(8,128)S(1)} %multiply_add_fusion.2), channel_id=1, source_target_pairs={{0,4},{4,8},{8,12},{12,16},{16,20},{20,24},{24,28},{28,32},{32,36}... | collective-permute-start | bytes 1966088 | tf_op jit(solution)/shard_map/while/body/eval_jaxpr/ppermute | solution.py:13
  623.9 20.8 %collective-permute-start = (f32[20,64,128]{2,1,0:T(8,128)S(1)}, f32[20,64,128]{2,1,0:T(8,128)S(1)}, u32[]{:S(2)}, u32[]{:S(2)}) collective-permute-start(f32[20,64,128]{2,1,0:T(8,128)S(1)} %multiply_add_fusion.2), channel_id=1, source_target_pairs={{0,4},{4,8},{8,12},{12,16},{16,20},{20,24},{24,28},{28,32},{32,36}... | collective-permute-start | bytes 1966088 | tf_op jit(solution)/shard_map/while/body/eval_jaxpr/ppermute | solution.py:13
  644.8 19.9 %collective-permute-start = (f32[20,64,128]{2,1,0:T(8,128)S(1)}, f32[20,64,128]{2,1,0:T(8,128)S(1)}, u32[]{:S(2)}, u32[]{:S(2)}) collective-permute-start(f32[20,64,128]{2,1,0:T(8,128)S(1)} %multiply_add_fusion.2), channel_id=1, source_target_pairs={{0,4},{4,8},{8,12},{12,16},{16,20},{20,24},{24,28},{28,32},{32,36}... | collective-permute-start | bytes 1966088 | tf_op jit(solution)/shard_map/while/body/eval_jaxpr/ppermute | solution.py:13
  664.8 19.0 %collective-permute-start = (f32[20,64,128]{2,1,0:T(8,128)S(1)}, f32[20,64,128]{2,1,0:T(8,128)S(1)}, u32[]{:S(2)}, u32[]{:S(2)}) collective-permute-start(f32[20,64,128]{2,1,0:T(8,128)S(1)} %multiply_add_fusion.2), channel_id=1, source_target_pairs={{0,4},{4,8},{8,12},{12,16},{16,20},{20,24},{24,28},{28,32},{32,36}... | collective-permute-start | bytes 1966088 | tf_op jit(solution)/shard_map/while/body/eval_jaxpr/ppermute | solution.py:13
  684.0 18.2 %collective-permute-start = (f32[20,64,128]{2,1,0:T(8,128)S(1)}, f32[20,64,128]{2,1,0:T(8,128)S(1)}, u32[]{:S(2)}, u32[]{:S(2)}) collective-permute-start(f32[20,64,128]{2,1,0:T(8,128)S(1)} %multiply_add_fusion.2), channel_id=1, source_target_pairs={{0,4},{4,8},{8,12},{12,16},{16,20},{20,24},{24,28},{28,32},{32,36}... | collective-permute-start | bytes 1966088 | tf_op jit(solution)/shard_map/while/body/eval_jaxpr/ppermute | solution.py:13
  702.3 17.3 %collective-permute-start = (f32[20,64,128]{2,1,0:T(8,128)S(1)}, f32[20,64,128]{2,1,0:T(8,128)S(1)}, u32[]{:S(2)}, u32[]{:S(2)}) collective-permute-start(f32[20,64,128]{2,1,0:T(8,128)S(1)} %multiply_add_fusion.2), channel_id=1, source_target_pairs={{0,4},{4,8},{8,12},{12,16},{16,20},{20,24},{24,28},{28,32},{32,36}... | collective-permute-start | bytes 1966088 | tf_op jit(solution)/shard_map/while/body/eval_jaxpr/ppermute | solution.py:13
  719.8 16.5 %collective-permute-start = (f32[20,64,128]{2,1,0:T(8,128)S(1)}, f32[20,64,128]{2,1,0:T(8,128)S(1)}, u32[]{:S(2)}, u32[]{:S(2)}) collective-permute-start(f32[20,64,128]{2,1,0:T(8,128)S(1)} %multiply_add_fusion.2), channel_id=1, source_target_pairs={{0,4},{4,8},{8,12},{12,16},{16,20},{20,24},{24,28},{28,32},{32,36}... | collective-permute-start | bytes 1966088 | tf_op jit(solution)/shard_map/while/body/eval_jaxpr/ppermute | solution.py:13
  736.4 15.6 %collective-permute-start = (f32[20,64,128]{2,1,0:T(8,128)S(1)}, f32[20,64,128]{2,1,0:T(8,128)S(1)}, u32[]{:S(2)}, u32[]{:S(2)}) collective-permute-start(f32[20,64,128]{2,1,0:T(8,128)S(1)} %multiply_add_fusion.2), channel_id=1, source_target_pairs={{0,4},{4,8},{8,12},{12,16},{16,20},{20,24},{24,28},{28,32},{32,36}... | collective-permute-start | bytes 1966088 | tf_op jit(solution)/shard_map/while/body/eval_jaxpr/ppermute | solution.py:13
  752.1 14.8 %collective-permute-start = (f32[20,64,128]{2,1,0:T(8,128)S(1)}, f32[20,64,128]{2,1,0:T(8,128)S(1)}, u32[]{:S(2)}, u32[]{:S(2)}) collective-permute-start(f32[20,64,128]{2,1,0:T(8,128)S(1)} %multiply_add_fusion.2), channel_id=1, source_target_pairs={{0,4},{4,8},{8,12},{12,16},{16,20},{20,24},{24,28},{28,32},{32,36}... | collective-permute-start | bytes 1966088 | tf_op jit(solution)/shard_map/while/body/eval_jaxpr/ppermute | solution.py:13
  767.0 15.7 %collective-permute-start = (f32[20,64,128]{2,1,0:T(8,128)S(1)}, f32[20,64,128]{2,1,0:T(8,128)S(1)}, u32[]{:S(2)}, u32[]{:S(2)}) collective-permute-start(f32[20,64,128]{2,1,0:T(8,128)S(1)} %multiply_add_fusion.2), channel_id=1, source_target_pairs={{0,4},{4,8},{8,12},{12,16},{16,20},{20,24},{24,28},{28,32},{32,36}... | collective-permute-start | bytes 1966088 | tf_op jit(solution)/shard_map/while/body/eval_jaxpr/ppermute | solution.py:13
  782.9 16.9 %collective-permute-start = (f32[20,64,128]{2,1,0:T(8,128)S(1)}, f32[20,64,128]{2,1,0:T(8,128)S(1)}, u32[]{:S(2)}, u32[]{:S(2)}) collective-permute-start(f32[20,64,128]{2,1,0:T(8,128)S(1)} %multiply_add_fusion.2), channel_id=1, source_target_pairs={{0,4},{4,8},{8,12},{12,16},{16,20},{20,24},{24,28},{28,32},{32,36}... | collective-permute-start | bytes 1966088 | tf_op jit(solution)/shard_map/while/body/eval_jaxpr/ppermute | solution.py:13
  799.9 18.0 %collective-permute-start = (f32[20,64,128]{2,1,0:T(8,128)S(1)}, f32[20,64,128]{2,1,0:T(8,128)S(1)}, u32[]{:S(2)}, u32[]{:S(2)}) collective-permute-start(f32[20,64,128]{2,1,0:T(8,128)S(1)} %multiply_add_fusion.2), channel_id=1, source_target_pairs={{0,4},{4,8},{8,12},{12,16},{16,20},{20,24},{24,28},{28,32},{32,36}... | collective-permute-start | bytes 1966088 | tf_op jit(solution)/shard_map/while/body/eval_jaxpr/ppermute | solution.py:13
  818.1 19.2 %collective-permute-start = (f32[20,64,128]{2,1,0:T(8,128)S(1)}, f32[20,64,128]{2,1,0:T(8,128)S(1)}, u32[]{:S(2)}, u32[]{:S(2)}) collective-permute-start(f32[20,64,128]{2,1,0:T(8,128)S(1)} %multiply_add_fusion.2), channel_id=1, source_target_pairs={{0,4},{4,8},{8,12},{12,16},{16,20},{20,24},{24,28},{28,32},{32,36}... | collective-permute-start | bytes 1966088 | tf_op jit(solution)/shard_map/while/body/eval_jaxpr/ppermute | solution.py:13
  837.4 20.3 %collective-permute-start = (f32[20,64,128]{2,1,0:T(8,128)S(1)}, f32[20,64,128]{2,1,0:T(8,128)S(1)}, u32[]{:S(2)}, u32[]{:S(2)}) collective-permute-start(f32[20,64,128]{2,1,0:T(8,128)S(1)} %multiply_add_fusion.2), channel_id=1, source_target_pairs={{0,4},{4,8},{8,12},{12,16},{16,20},{20,24},{24,28},{28,32},{32,36}... | collective-permute-start | bytes 1966088 | tf_op jit(solution)/shard_map/while/body/eval_jaxpr/ppermute | solution.py:13
  857.8 21.5 %collective-permute-start = (f32[20,64,128]{2,1,0:T(8,128)S(1)}, f32[20,64,128]{2,1,0:T(8,128)S(1)}, u32[]{:S(2)}, u32[]{:S(2)}) collective-permute-start(f32[20,64,128]{2,1,0:T(8,128)S(1)} %multiply_add_fusion.2), channel_id=1, source_target_pairs={{0,4},{4,8},{8,12},{12,16},{16,20},{20,24},{24,28},{28,32},{32,36}... | collective-permute-start | bytes 1966088 | tf_op jit(solution)/shard_map/while/body/eval_jaxpr/ppermute | solution.py:13
  879.4 20.8 %collective-permute-start = (f32[20,64,128]{2,1,0:T(8,128)S(1)}, f32[20,64,128]{2,1,0:T(8,128)S(1)}, u32[]{:S(2)}, u32[]{:S(2)}) collective-permute-start(f32[20,64,128]{2,1,0:T(8,128)S(1)} %multiply_add_fusion.2), channel_id=1, source_target_pairs={{0,4},{4,8},{8,12},{12,16},{16,20},{20,24},{24,28},{28,32},{32,36}... | collective-permute-start | bytes 1966088 | tf_op jit(solution)/shard_map/while/body/eval_jaxpr/ppermute | solution.py:13
  900.3 19.9 %collective-permute-start = (f32[20,64,128]{2,1,0:T(8,128)S(1)}, f32[20,64,128]{2,1,0:T(8,128)S(1)}, u32[]{:S(2)}, u32[]{:S(2)}) collective-permute-start(f32[20,64,128]{2,1,0:T(8,128)S(1)} %multiply_add_fusion.2), channel_id=1, source_target_pairs={{0,4},{4,8},{8,12},{12,16},{16,20},{20,24},{24,28},{28,32},{32,36}... | collective-permute-start | bytes 1966088 | tf_op jit(solution)/shard_map/while/body/eval_jaxpr/ppermute | solution.py:13
  920.4 19.0 %collective-permute-start = (f32[20,64,128]{2,1,0:T(8,128)S(1)}, f32[20,64,128]{2,1,0:T(8,128)S(1)}, u32[]{:S(2)}, u32[]{:S(2)}) collective-permute-start(f32[20,64,128]{2,1,0:T(8,128)S(1)} %multiply_add_fusion.2), channel_id=1, source_target_pairs={{0,4},{4,8},{8,12},{12,16},{16,20},{20,24},{24,28},{28,32},{32,36}... | collective-permute-start | bytes 1966088 | tf_op jit(solution)/shard_map/while/body/eval_jaxpr/ppermute | solution.py:13
  939.5 18.2 %collective-permute-start = (f32[20,64,128]{2,1,0:T(8,128)S(1)}, f32[20,64,128]{2,1,0:T(8,128)S(1)}, u32[]{:S(2)}, u32[]{:S(2)}) collective-permute-start(f32[20,64,128]{2,1,0:T(8,128)S(1)} %multiply_add_fusion.2), channel_id=1, source_target_pairs={{0,4},{4,8},{8,12},{12,16},{16,20},{20,24},{24,28},{28,32},{32,36}... | collective-permute-start | bytes 1966088 | tf_op jit(solution)/shard_map/while/body/eval_jaxpr/ppermute | solution.py:13
  957.9 17.3 %collective-permute-start = (f32[20,64,128]{2,1,0:T(8,128)S(1)}, f32[20,64,128]{2,1,0:T(8,128)S(1)}, u32[]{:S(2)}, u32[]{:S(2)}) collective-permute-start(f32[20,64,128]{2,1,0:T(8,128)S(1)} %multiply_add_fusion.2), channel_id=1, source_target_pairs={{0,4},{4,8},{8,12},{12,16},{16,20},{20,24},{24,28},{28,32},{32,36}... | collective-permute-start | bytes 1966088 | tf_op jit(solution)/shard_map/while/body/eval_jaxpr/ppermute | solution.py:13
  975.3 16.5 %collective-permute-start = (f32[20,64,128]{2,1,0:T(8,128)S(1)}, f32[20,64,128]{2,1,0:T(8,128)S(1)}, u32[]{:S(2)}, u32[]{:S(2)}) collective-permute-start(f32[20,64,128]{2,1,0:T(8,128)S(1)} %multiply_add_fusion.2), channel_id=1, source_target_pairs={{0,4},{4,8},{8,12},{12,16},{16,20},{20,24},{24,28},{28,32},{32,36}... | collective-permute-start | bytes 1966088 | tf_op jit(solution)/shard_map/while/body/eval_jaxpr/ppermute | solution.py:13
  991.9 14.6 %collective-permute-start = (f32[20,64,128]{2,1,0:T(8,128)S(1)}, f32[20,64,128]{2,1,0:T(8,128)S(1)}, u32[]{:S(2)}, u32[]{:S(2)}) collective-permute-start(f32[20,64,128]{2,1,0:T(8,128)S(1)} %multiply_add_fusion.2), channel_id=1, source_target_pairs={{0,4},{4,8},{8,12},{12,16},{16,20},{20,24},{24,28},{28,32},{32,36}... | collective-permute-start | bytes 1966088 | tf_op jit(solution)/shard_map/while/body/eval_jaxpr/ppermute | solution.py:13
  1006.7 14.6 %collective-permute-start = (f32[20,64,128]{2,1,0:T(8,128)S(1)}, f32[20,64,128]{2,1,0:T(8,128)S(1)}, u32[]{:S(2)}, u32[]{:S(2)}) collective-permute-start(f32[20,64,128]{2,1,0:T(8,128)S(1)} %multiply_add_fusion.2), channel_id=1, source_target_pairs={{0,4},{4,8},{8,12},{12,16},{16,20},{20,24},{24,28},{28,32},{32,36}... | collective-permute-start | bytes 1966088 | tf_op jit(solution)/shard_map/while/body/eval_jaxpr/ppermute | solution.py:13
  1021.2 4.2 copy-start
  1021.2 4.3 copy-start.7
